TPU v7x, 128 devices: a whole 4x4x4 slice. The times are simulated.
128 devices in a mesh: row: 8 (over z, core), col: 16 (over x, y).
Axes of the slice: x: 4, y: 4, z: 4, core: 2. Of those that a mesh axis runs over, the one named last changes fastest.
Arguments:
- recorded: bfloat16 [2048, 64, 3072], P(('row', 'col')), may hold values from -6 to 6
- seg_count: int32 [128], P(('row', 'col')), may hold values from 0 to 16, as said below
- slot_station: int32 [2048], P(('row', 'col')), may hold values from 0 to 1023, as said below
- window_mask: int32 [1024, 64], P(('row', 'col')), may hold values from 0 to 1, as said below
Outputs:
- cross_real: bfloat16 [1024, 1024, 384], P('row', 'col')
- cross_imag: bfloat16 [1024, 1024, 384], P('row', 'col')
Inputs may be any that keep to these rules, and one draw needn't show every extreme that they name: `seg_count`: recorder d = r * 16 + c serves row r of the grid; in every row exactly half of the 16 recorders have 16 live slots and the others none. `slot_station`: the live slots of the recorders of row r name each station of r * 128 to (r + 1) * 128 - 1 exactly once; a recorder's live slots name 2 or no stations of each owner (stations with equal s // 8); dead slots name arbitrary stations. `window_mask`: A station's invalid windows form one cyclic run of 0 to 64 windows.
All inputs are finite; a program needn't handle non-finite values.
Results may differ from a plain program's by a relative error of at most 0.0066.
Values may be sent and summed in bfloat16 or wider, within the bound.
No kernel may reach another device: no remote copies, remote signals or barrier semaphores. Data moves between devices by JAX's collectives and lax.ppermute only.
A program may use at most 128 MiB of HBM per device.

v0:
```python
import math

import jax
import jax.numpy as jnp
from jax import lax
from jax.sharding import PartitionSpec as P

F = 384
L = 3072
F0 = 13
BAND = 64
CAP = 2
W = 64


def transform_table():
    times = jnp.arange(L, dtype=jnp.int32)
    freqs = jnp.arange(F, dtype=jnp.int32) + F0
    phase = times[:, None] * freqs[None, :] % L
    angle = phase.astype(jnp.float32) * (2.0 * math.pi / L)
    return jnp.concatenate([jnp.cos(angle), -jnp.sin(angle)], axis=1).astype(jnp.bfloat16)


def whiten(segments, table):
    count = segments.shape[0]
    spectrum = jnp.dot(segments.reshape(count * W, L), table, preferred_element_type=jnp.float32)
    real = spectrum[:, :F]
    imag = spectrum[:, F:]
    power = (real * real + imag * imag).reshape(count * W, F // BAND, BAND)
    factor = lax.rsqrt(jnp.mean(power, axis=2) + 1e-05)
    factor = jnp.repeat(factor, BAND, axis=1)
    white = jnp.concatenate([real * factor, imag * factor], axis=1)
    return white.astype(jnp.bfloat16).reshape(count, W, 2 * F)


def per_device(recorded, seg_count, slot_station, window_mask):
    columns = lax.axis_size("col")
    slots_here = recorded.shape[0]
    owned = window_mask.shape[0]
    outgoing = columns * CAP
    slot_index = jnp.arange(slots_here, dtype=jnp.int32)
    live = slot_index < seg_count[0]
    target_col = jnp.where(live, slot_station // owned % columns, columns)
    onehot = (target_col[:, None] == jnp.arange(columns, dtype=jnp.int32)[None, :]).astype(
        jnp.int32
    )
    earlier = jnp.cumsum(onehot, axis=0) - onehot
    rank = jnp.sum(earlier * onehot, axis=1)
    position = jnp.where(live, target_col * CAP + rank, outgoing)
    chosen = position[None, :] == jnp.arange(outgoing, dtype=jnp.int32)[:, None]
    source = jnp.sum(jnp.where(chosen, slot_index[None, :], 0), axis=1)
    local_id = jnp.sum(jnp.where(chosen, slot_station[None, :] % owned + 1, 0), axis=1) - 1
    labels = local_id.astype(jnp.bfloat16).reshape(columns, CAP)
    table = transform_table()
    payload = jnp.take(recorded, source, axis=0).reshape(columns, CAP, W, L)
    arrived, tags = (
        lax.all_to_all(payload, "col", split_axis=0, concat_axis=0, tiled=True),
        lax.all_to_all(labels, "col", split_axis=0, concat_axis=0, tiled=True),
    )
    tags = tags.reshape(outgoing).astype(jnp.int32)
    flat = arrived.reshape(outgoing, W, arrived.shape[3])
    match = tags[None, :] == jnp.arange(owned, dtype=jnp.int32)[:, None]
    pick = jnp.sum(jnp.where(match, jnp.arange(outgoing, dtype=jnp.int32)[None, :], 0), axis=1)
    mine = jnp.take(flat, pick, axis=0)
    spectra = whiten(mine, table)
    mask_float = window_mask.astype(jnp.bfloat16)
    spectra = spectra * mask_float[:, :, None]
    stacked = spectra.reshape(owned, W, 2, F).transpose(3, 0, 2, 1).reshape(F, owned, 2 * W)
    left, left_mask = (
        lax.all_gather(stacked, "col", axis=1, tiled=True),
        lax.all_gather(mask_float, "col", axis=0, tiled=True),
    )
    right, right_mask = (
        lax.all_gather(stacked, "row", axis=1, tiled=True),
        lax.all_gather(mask_float, "row", axis=0, tiled=True),
    )
    counts = jnp.dot(left_mask, right_mask.T, preferred_element_type=jnp.float32)
    inverse = 1.0 / jnp.maximum(counts, 1.0)
    across = right.shape[1]
    turned = jnp.concatenate([right[:, :, W:], -right[:, :, :W]], axis=2)
    both = jnp.concatenate([right, turned], axis=1)
    product = jnp.einsum("fiw,fjw->ijf", left, both, preferred_element_type=jnp.float32)
    real_part = (product[:, :across, :] * inverse[:, :, None]).astype(jnp.bfloat16)
    imag_part = (product[:, across:, :] * inverse[:, :, None]).astype(jnp.bfloat16)
    return (real_part, imag_part)


def solution(mesh):
    placed = (
        P(("row", "col"), None, None),
        P(("row", "col")),
        P(("row", "col")),
        P(("row", "col"), None),
    )
    return jax.shard_map(
        per_device,
        mesh=mesh,
        in_specs=placed,
        out_specs=(P("row", "col", None), P("row", "col", None)),
        check_vma=False,
    )
```

profile of v0, /device:TPU:0, one launch (start us, length us, event | category | flops | bytes accessed | tf_op | source)
XLA Modules:
  0.0 494.6 jit_solution(11430254378212327538)
XLA Ops:
  7.8 0.7 compare_select_fusion.10
  8.5 0.1 fusion.21
  8.6 0.2 select_reduce_fusion.2
  8.8 0.1 select_reduce_fusion.1
  8.9 0.7 convert_element_type.55
  9.6 7.1 %all-to-all-start = ((bf16[16,1,2]{2,1,0:T(2,128)(2,1)}), bf16[16,1,2]{2,1,0:T(2,128)(2,1)S(1)}, u32[]{:S(2)}, u32[]{:S(2)}) async-start(bf16[16,1,2]{2,1,0:T(2,128)(2,1)} %convert_element_type.55), calls=%async_computation | async-start | bytes 16384 | tf_op jit(solution)/shard_map/all_to_all | solution.py:58
  16.8 0.1 reduce_sum.55
  16.9 9.0 %gather_fusion = bf16[32,64,3072]{2,1,0:T(8,128)(2,1)} fusion(bf16[16,64,3072]{2,1,0:T(8,128)(2,1)} %param.4, s32[1024]{0:T(1024)S(1)} %pad_clamp_fusion.1), kind=kCustom, calls=%fused_computation | custom fusion | bytes 25165952 | tf_op jit(solution)/shard_map/jit(_take)/gather | solution.py:55
  25.9 10.9 %broadcast_select_fusion = bf16[16,2,64,3072]{3,2,1,0:T(8,128)(2,1)} fusion(bf16[16,2,64,3072]{3,2,1,0:T(8,128)(2,1)} %bitcast.32, pred[16,2]{1,0:T(8,128)(4,1)S(1)} %compare_and_fusion), kind=kLoop, calls=%fused_computation.12 | loop fusion | flops 6291456 | bytes 25165856 | tf_op jit(solution)/shard_map/jit(_take)/select_n | solution.py:55
  36.8 0.0 copy-start.2
  36.8 0.0 all-to-all-done
  36.8 7.4 %all-to-all-start.1 = ((bf16[16,2,64,3072]{3,2,1,0:T(8,128)(2,1)}), bf16[16,2,64,3072]{3,2,1,0:T(8,128)(2,1)}, u32[]{:S(2)}, u32[]{:S(2)}) async-start(bf16[16,2,64,3072]{3,2,1,0:T(8,128)(2,1)} %broadcast_select_fusion), calls=%async_computation.1 | async-start | bytes 25165824 | tf_op jit(solution)/shard_map/all_to_all | solution.py:57
  44.2 0.0 all-gather.3.cloned.1.call-start
  44.3 0.0 copy-done.2
  44.3 21.0 %cosine_convert_fusion = (bf16[3072,384]{1,0:T(8,128)(2,1)}, bf16[3072,384]{1,0:T(8,128)(2,1)}) fusion(s32[384]{0:T(512)S(1)} %iota_add_fusion), kind=kLoop, calls=%fused_computation.23 | loop fusion | flops 14155776 | bytes 4720128 | tf_op jit(solution)/shard_map/convert.5
  65.3 0.1 reshape.118
  65.4 0.1 select_reduce_fusion.3
  65.5 0.1 broadcast_in_dim.81
  65.6 0.1 broadcast_in_dim.82
  65.7 198.4 %all-to-all-done.1 = bf16[16,2,64,3072]{3,2,1,0:T(8,128)(2,1)} async-done(((bf16[16,2,64,3072]{3,2,1,0:T(8,128)(2,1)}), bf16[16,2,64,3072]{3,2,1,0:T(8,128)(2,1)}, u32[]{:S(2)}, u32[]{:S(2)}) %all-to-all-start.1) | async-done | bytes 12582944 | tf_op jit(solution)/shard_map/all_to_all | solution.py:57
  264.1 5.3 %gather_fusion.1 = bf16[8,64,3072]{2,1,0:T(8,128)(2,1)S(1)} fusion(bf16[32,64,3072]{2,1,0:T(8,128)(2,1)} %bitcast.4, s32[1024]{0:T(1024)S(1)} %pad_clamp_fusion), kind=kCustom, calls=%fused_computation.1 | custom fusion | bytes 6291488 | tf_op jit(solution)/shard_map/jit(_take)/gather | solution.py:64
  269.4 0.0 copy-start
  269.5 0.0 copy-start.1
  269.5 0.5 bitcast_select_fusion
  270.0 1.1 copy-done
  271.1 0.7 copy-done.1
  271.8 2.6 fusion.13
  274.4 0.1 multiply_add_fusion
  274.5 0.3 copy.29
  274.8 0.1 reduce_sum.58
  274.9 0.1 broadcast_in_dim.88
  275.0 0.3 copy.30
  275.3 0.2 multiply_convert_fusion.1
  275.5 0.2 maximum_multiply_fusion
  275.6 1.3 copy.34
  277.0 0.0 all-gather.3.cloned.1.call-update
  277.0 0.0 all-gather.5.cloned.1.call-start
  277.1 0.7 all-gather.5.cloned.1.call-update
  277.8 12.8 %all_gather.15 = bf16[64,64]{1,0:T(8,128)(2,1)S(1)} all-gather(bf16[8,64]{1,0:T(8,128)(2,1)S(1)} %convert_element_type.51), channel_id=1, replica_groups=mesh['row'=8,'col'=16] {'row'}, dimensions={0}, use_global_device_ids=true | all-gather | bytes 9216 | tf_op jit(solution)/shard_map/all_gather | solution.py:75
  290.6 26.5 %all_gather.14 = bf16[128,64]{1,0:T(8,128)(2,1)S(1)} all-gather(bf16[8,64]{1,0:T(8,128)(2,1)S(1)} %convert_element_type.51), channel_id=1, replica_groups=mesh['row'=8,'col'=16] {'col'}, dimensions={0}, use_global_device_ids=true | all-gather | bytes 17408 | tf_op jit(solution)/shard_map/all_gather | solution.py:71
  317.1 0.2 fusion.20
  317.3 11.8 %all-gather.3.cloned.1.call-done = bf16[384,64,128]{2,1,0:T(8,128)(2,1)} async-done(((bf16[384,8,128]{2,1,0:T(8,128)(2,1)}), bf16[384,64,128]{2,1,0:T(8,128)(2,1)}) %all-gather.3.cloned.1.call-update) | async-done | bytes 6291472 | tf_op jit(solution)/shard_map/all_gather | solution.py:74
  329.1 11.9 %fusion.28 = (bf16[384,64,64]{2,1,0:T(8,128)(2,1)}, bf16[384,64,64]{2,1,0:T(8,128)(2,1)}) fusion(bf16[384,64,128]{2,1,0:T(8,128)(2,1)} %all-gather.3.cloned.1.call-done), kind=kLoop, calls=%fused_computation.71 | loop fusion | flops 1572864 | bytes 12582912 | tf_op jit(solution)/shard_map/slice | solution.py:80
  341.0 89.4 %all-gather.5.cloned.1.call-done = bf16[384,128,128]{2,1,0:T(8,128)(2,1)} async-done(((bf16[384,8,128]{2,1,0:T(8,128)(2,1)}), bf16[384,128,128]{2,1,0:T(8,128)(2,1)}) %all-gather.5.cloned.1.call-update) | async-done | bytes 12582928 | tf_op jit(solution)/shard_map/all_gather | solution.py:70
  430.4 23.3 %fusion.8 = f32[128,128,384]{0,1,2:T(8,128)} fusion(bf16[384,128,128]{2,1,0:T(8,128)(2,1)} %all-gather.5.cloned.1.call-done, bf16[384,64,64]{2,1,0:T(8,128)(2,1)} %get-tuple-element.15, bf16[384,64,64]{2,1,0:T(8,128)(2,1)} %get-tuple-element.14, bf16[384,64,128]{2,1,0:T(8,128)(2,1)} %all-gather.3.cloned.1.call-done), kind=kOutput, calls=%fused_computation.13 | convolution fusion | flops 1648361472 | bytes 50331648 | tf_op jit(solution)/shard_map/fiw,fjw->ijf/dot_general | solution.py:82
  453.7 14.7 %fusion = (bf16[128,64,384]{0,1,2:T(8,128)(2,1)}, bf16[128,64,384]{0,1,2:T(8,128)(2,1)}) fusion(f32[128,128,384]{0,1,2:T(8,128)} %fusion.8, f32[128,64]{0,1:T(8,128)S(1)} %fusion.20), kind=kLoop, calls=%fused_computation.3 | loop fusion | flops 12582912 | bytes 37781504 | tf_op jit(solution)/shard_map/convert_element_type | solution.py:84
  468.4 9.7 %copy.36 = bf16[128,64,384]{2,1,0:T(8,128)(2,1)} copy(bf16[128,64,384]{0,1,2:T(8,128)(2,1)} %get-tuple-element.13) | data formatting | bytes 12582912
  478.1 9.7 %copy.37 = bf16[128,64,384]{2,1,0:T(8,128)(2,1)} copy(bf16[128,64,384]{0,1,2:T(8,128)(2,1)} %get-tuple-element.12) | data formatting | bytes 12582912
  (13 shorter events, 0.1 us)
Async XLA Ops:
  9.6 27.2 %all-to-all-start = ((bf16[16,1,2]{2,1,0:T(2,128)(2,1)}), bf16[16,1,2]{2,1,0:T(2,128)(2,1)S(1)}, u32[]{:S(2)}, u32[]{:S(2)}) async-start(bf16[16,1,2]{2,1,0:T(2,128)(2,1)} %convert_element_type.55), calls=%async_computation | async-start | bytes 16384 | tf_op jit(solution)/shard_map/all_to_all | solution.py:58
  36.8 7.5 %copy-start.2 = (s32[8,64]{1,0:T(8,128)S(1)}, s32[8,64]{1,0:T(8,128)}, u32[]{:S(2)}) copy-start(s32[8,64]{1,0:T(8,128)} %param.7) | copy-start | bytes 6148
  36.8 227.3 %all-to-all-start.1 = ((bf16[16,2,64,3072]{3,2,1,0:T(8,128)(2,1)}), bf16[16,2,64,3072]{3,2,1,0:T(8,128)(2,1)}, u32[]{:S(2)}, u32[]{:S(2)}) async-start(bf16[16,2,64,3072]{3,2,1,0:T(8,128)(2,1)} %broadcast_select_fusion), calls=%async_computation.1 | async-start | bytes 25165824 | tf_op jit(solution)/shard_map/all_to_all | solution.py:57
  44.2 284.9 %all-gather.3.cloned.1.call-start = ((), (), s32[]{:S(2)}) async-start(), calls=%async_computation.2 | async-start | bytes 7077888 | tf_op jit(solution)/shard_map/all_gather | solution.py:74
  269.4 1.7 copy-start
  269.5 2.4 copy-start.1
  277.0 153.4 %all-gather.5.cloned.1.call-start = ((), (), s32[]{:S(2)}) async-start(), calls=%async_computation.3 | async-start | bytes 13369344 | tf_op jit(solution)/shard_map/all_gather | solution.py:70
Sparse Core Ops, SparseCore 0:
  277.1 51.9 all-gather.2
  331.2 99.0 all-gather.4
where the time goes:
time: 495 us
  waiting for transfers between devices  300 us (61%)
  other arithmetic  60.7 us (12%)
  blocking collectives  39.4 us (8%)
  local copies, waits for them, and re-layouts  38.6 us (8%)
  matrix products  26.1 us (5%)
  between operations  14.9 us (3%)
  starting transfers between devices  14.6 us (3%)
    all_to_all x1, waiting for transfers between devices, per_device(): lax.all_to_all(payload, 'col', split_axis=0, concat_axis=0, tiled=True)  198 us
    all_gather x1, waiting for transfers between devices, per_device(): lax.all_gather(stacked, 'col', axis=1, tiled=True)  89.4 us
    all_gather x1, blocking collectives, per_device(): lax.all_gather(mask_float, 'col', axis=0, tiled=True)  26.5 us
    dot_general x1, matrix products, per_device(): jnp.einsum('fiw,fjw->ijf', left, both, preferred_element_type=jnp.float32)  23.3 us
    unnamed x8, local copies, waits for them, and re-layouts  21.2 us
    another operation x2, other arithmetic  21.1 us
    convert_element_type x1, other arithmetic, per_device(): (product[:, across:, :] * inverse[:, :, None]).astype(jnp.bfloat16)  14.7 us
    all_gather x1, blocking collectives, per_device(): lax.all_gather(mask_float, 'row', axis=0, tiled=True)  12.8 us
  transfers between devices with their start and end apart: 4, of which 3 were waited for; matrix products, arithmetic and copies ran while one was open for 11% of the time, Pallas kernels for 0%

commit v1 on v0

--- a/solution.py
+++ b/solution.py
@@ -14,11 +14,17 @@
 
 
 def transform_table():
-    times = jnp.arange(L, dtype=jnp.int32)
     freqs = jnp.arange(F, dtype=jnp.int32) + F0
-    phase = times[:, None] * freqs[None, :] % L
-    angle = phase.astype(jnp.float32) * (2.0 * math.pi / L)
-    return jnp.concatenate([jnp.cos(angle), -jnp.sin(angle)], axis=1).astype(jnp.bfloat16)
+    high = jnp.arange(L // 64, dtype=jnp.int32)[:, None] * 64 * freqs[None, :] % L
+    low = jnp.arange(64, dtype=jnp.int32)[:, None] * freqs[None, :] % L
+    scale = 2.0 * math.pi / L
+    ah = high.astype(jnp.float32) * scale
+    al = low.astype(jnp.float32) * scale
+    ch, sh = jnp.cos(ah)[:, None, :], jnp.sin(ah)[:, None, :]
+    cl, sl = jnp.cos(al)[None, :, :], jnp.sin(al)[None, :, :]
+    cos_part = (ch * cl - sh * sl).reshape(L, F)
+    sin_part = (sh * cl + ch * sl).reshape(L, F)
+    return jnp.concatenate([cos_part, -sin_part], axis=1).astype(jnp.bfloat16)
 
 
 def whiten(segments, table):
@@ -52,7 +58,8 @@
     local_id = jnp.sum(jnp.where(chosen, slot_station[None, :] % owned + 1, 0), axis=1) - 1
     labels = local_id.astype(jnp.bfloat16).reshape(columns, CAP)
     table = transform_table()
-    payload = jnp.take(recorded, source, axis=0).reshape(columns, CAP, W, L)
+    local_white = whiten(recorded, table)
+    payload = jnp.take(local_white, source, axis=0).reshape(columns, CAP, W, 2 * F)
     arrived, tags = (
         lax.all_to_all(payload, "col", split_axis=0, concat_axis=0, tiled=True),
         lax.all_to_all(labels, "col", split_axis=0, concat_axis=0, tiled=True),
@@ -61,8 +68,7 @@
     flat = arrived.reshape(outgoing, W, arrived.shape[3])
     match = tags[None, :] == jnp.arange(owned, dtype=jnp.int32)[:, None]
     pick = jnp.sum(jnp.where(match, jnp.arange(outgoing, dtype=jnp.int32)[None, :], 0), axis=1)
-    mine = jnp.take(flat, pick, axis=0)
-    spectra = whiten(mine, table)
+    spectra = jnp.take(flat, pick, axis=0)
     mask_float = window_mask.astype(jnp.bfloat16)
     spectra = spectra * mask_float[:, :, None]
     stacked = spectra.reshape(owned, W, 2, F).transpose(3, 0, 2, 1).reshape(F, owned, 2 * W)

time: 495 us -> 308 us (0.62)
  waiting for transfers between devices: 300 us -> 142 us
  other arithmetic: 60.7 us -> 40.3 us
  local copies, waits for them, and re-layouts: 38.6 us -> 30.6 us
  blocking collectives: 39.4 us -> 33.9 us
    all_to_all x1, waiting for transfers between devices: 198 us -> 42.3 us  [per_device(): lax.all_to_all(payload, 'col', split_axis=0, concat_axis=0, tiled=True)]
    another operation x2, other arithmetic: 21.1 us -> 3.55 us
    gather x2 -> x3, local copies, waits for them, and re-layouts: 14.4 us -> 5.94 us  [the longest x2 3.53 us: per_device(): spectra = jnp.take(flat, pick, axis=0)]
    select_n x4 -> x3, other arithmetic: 11.4 us -> 3.93 us  [the longest x2 3.92 us: per_device(): jnp.take(local_white, source, axis=0).reshape(columns, CAP, W, 2 * F)]
    all_gather x1, blocking collectives: 26.5 us -> 21.1 us  [per_device(): lax.all_gather(mask_float, 'col', axis=0, tiled=True)]
    unnamed x8 -> x4, local copies, waits for them, and re-layouts: 21.2 us -> 19.4 us
  transfers between devices with their start and end apart: 4 -> 4, of which waited for: 3 -> 3; matrix products, arithmetic and copies ran while one was open for 11% -> 12% of each run, Pallas kernels for 0% -> 0%
where the time goes in v1:
time: 308 us; the launch traced here: 307 us
  waiting for transfers between devices  142 us (46%)
  other arithmetic  40.3 us (13%)
  blocking collectives  33.9 us (11%)
  matrix products  30.8 us (10%)
  local copies, waits for them, and re-layouts  30.6 us (10%)
  between operations  14.9 us (5%)
  starting transfers between devices  14.6 us (5%)
    all_gather x1, waiting for transfers between devices, per_device(): lax.all_gather(stacked, 'col', axis=1, tiled=True)  89.4 us
    all_to_all x1, waiting for transfers between devices, per_device(): lax.all_to_all(payload, 'col', split_axis=0, concat_axis=0, tiled=True)  42.3 us
    dot_general x1, matrix products, per_device(): jnp.einsum('fiw,fjw->ijf', left, both, preferred_element_type=jnp.float32)  23.3 us
    all_gather x1, blocking collectives, per_device(): lax.all_gather(mask_float, 'col', axis=0, tiled=True)  21.1 us
    unnamed x4, local copies, waits for them, and re-layouts  19.4 us
    convert_element_type x1, other arithmetic, per_device(): (product[:, across:, :] * inverse[:, :, None]).astype(jnp.bfloat16)  14.7 us
    all_gather x1, blocking collectives, per_device(): lax.all_gather(mask_float, 'row', axis=0, tiled=True)  12.9 us
    slice x1, other arithmetic, per_device(): turned = jnp.concatenate([right[:, :, W:], -right[:, :, :W]], axis=2)  11.9 us
  transfers between devices with their start and end apart: 4, of which 3 were waited for; matrix products, arithmetic and copies ran while one was open for 12% of the time, Pallas kernels for 0%

profile of v1, /device:TPU:0, one launch (start us, length us, event | category | flops | bytes accessed | tf_op | source)
XLA Modules:
  0.0 306.7 jit_solution(5390992266270219547)
XLA Ops:
  7.8 0.7 compare_select_fusion.10
  8.5 0.1 fusion.35
  8.6 0.2 select_reduce_fusion.2
  8.8 0.1 select_reduce_fusion.1
  8.9 0.7 convert_element_type.74
  9.6 7.1 %all-to-all-start = ((bf16[16,1,2]{2,1,0:T(2,128)(2,1)}), bf16[16,1,2]{2,1,0:T(2,128)(2,1)S(1)}, u32[]{:S(2)}, u32[]{:S(2)}) async-start(bf16[16,1,2]{2,1,0:T(2,128)(2,1)} %convert_element_type.74), calls=%async_computation | async-start | bytes 16384 | tf_op jit(solution)/shard_map/all_to_all | solution.py:65
  16.8 0.1 reduce_sum.55
  16.9 0.4 fusion.26
  17.3 0.4 fusion.33
  17.7 2.0 subtract_convert_fusion
  19.7 7.3 %fusion.15 = f32[1024,768]{0,1:T(8,128)S(1)} fusion(bf16[1024,3072]{1,0:T(8,128)(2,1)} %bitcast.45, bf16[3072,384]{1,0:T(8,128)(2,1)S(1)} %bitcast.44, bf16[3072,384]{1,0:T(8,128)(2,1)S(1)} %bitcast.43), kind=kOutput, calls=%fused_computation.23 | convolution fusion | flops 4841275392 | bytes 14155776 | tf_op jit(solution)/shard_map/dot_general | solution.py:32
  27.0 1.5 multiply_add_fusion
  28.4 1.6 reduce_sum.56
  30.0 1.6 fusion.18
  31.6 1.5 copy.24
  33.1 1.5 copy.25
  34.6 0.2 pad_maximum_fusion
  34.8 2.4 gather_fusion
  37.2 3.9 %broadcast_select_fusion = bf16[16,2,64,768]{3,2,1,0:T(8,128)(2,1)} fusion(bf16[16,2,64,768]{3,2,1,0:T(8,128)(2,1)} %bitcast.37, pred[16,2]{1,0:T(8,128)(4,1)S(1)} %compare_and_fusion), kind=kLoop, calls=%fused_computation.20 | loop fusion | flops 1572864 | bytes 6291488 | tf_op jit(solution)/shard_map/jit(_take)/select_n | solution.py:62
  41.1 0.0 copy-start
  41.1 0.0 all-to-all-done
  41.1 7.4 %all-to-all-start.1 = ((bf16[16,2,64,768]{3,2,1,0:T(8,128)(2,1)}), bf16[16,2,64,768]{3,2,1,0:T(8,128)(2,1)S(1)}, u32[]{:S(2)}, u32[]{:S(2)}) async-start(bf16[16,2,64,768]{3,2,1,0:T(8,128)(2,1)} %broadcast_select_fusion), calls=%async_computation.1 | async-start | bytes 6291456 | tf_op jit(solution)/shard_map/all_to_all | solution.py:64
  48.5 0.0 all-gather.3.cloned.1.call-start
  48.5 0.0 copy-done
  48.6 0.1 reshape.243
  48.7 0.1 select_reduce_fusion.3
  48.8 42.3 %all-to-all-done.1 = bf16[16,2,64,768]{3,2,1,0:T(8,128)(2,1)S(1)} async-done(((bf16[16,2,64,768]{3,2,1,0:T(8,128)(2,1)}), bf16[16,2,64,768]{3,2,1,0:T(8,128)(2,1)S(1)}, u32[]{:S(2)}, u32[]{:S(2)}) %all-to-all-start.1) | async-done | bytes 3145760 | tf_op jit(solution)/shard_map/all_to_all | solution.py:64
  91.1 1.5 gather_fusion.1
  92.6 2.1 gather.15
  94.6 1.0 multiply_bitcast_fusion
  95.7 0.1 copy.26
  95.8 1.3 copy.27
  97.2 0.0 all-gather.3.cloned.1.call-update
  97.2 0.0 all-gather.5.cloned.1.call-start
  97.2 0.7 all-gather.5.cloned.1.call-update
  97.9 12.9 %all_gather.15 = bf16[64,64]{1,0:T(8,128)(2,1)S(1)} all-gather(bf16[8,64]{1,0:T(8,128)(2,1)S(1)} %convert_element_type.70), channel_id=1, replica_groups=mesh['row'=8,'col'=16] {'row'}, dimensions={0}, use_global_device_ids=true | all-gather | bytes 9216 | tf_op jit(solution)/shard_map/all_gather | solution.py:81
  110.8 21.1 %all_gather.14 = bf16[128,64]{1,0:T(8,128)(2,1)S(1)} all-gather(bf16[8,64]{1,0:T(8,128)(2,1)S(1)} %convert_element_type.70), channel_id=1, replica_groups=mesh['row'=8,'col'=16] {'col'}, dimensions={0}, use_global_device_ids=true | all-gather | bytes 17408 | tf_op jit(solution)/shard_map/all_gather | solution.py:77
  131.9 0.2 fusion.20
  132.1 9.2 %all-gather.3.cloned.1.call-done = bf16[384,64,128]{2,1,0:T(8,128)(2,1)} async-done(((bf16[384,8,128]{2,1,0:T(8,128)(2,1)}), bf16[384,64,128]{2,1,0:T(8,128)(2,1)}) %all-gather.3.cloned.1.call-update) | async-done | bytes 6291472 | tf_op jit(solution)/shard_map/all_gather | solution.py:80
  141.3 11.9 %fusion.42 = (bf16[384,64,64]{2,1,0:T(8,128)(2,1)}, bf16[384,64,64]{2,1,0:T(8,128)(2,1)}) fusion(bf16[384,64,128]{2,1,0:T(8,128)(2,1)} %all-gather.3.cloned.1.call-done), kind=kLoop, calls=%fused_computation.87 | loop fusion | flops 1572864 | bytes 12582912 | tf_op jit(solution)/shard_map/slice | solution.py:86
  153.1 89.4 %all-gather.5.cloned.1.call-done = bf16[384,128,128]{2,1,0:T(8,128)(2,1)} async-done(((bf16[384,8,128]{2,1,0:T(8,128)(2,1)}), bf16[384,128,128]{2,1,0:T(8,128)(2,1)}) %all-gather.5.cloned.1.call-update) | async-done | bytes 12582928 | tf_op jit(solution)/shard_map/all_gather | solution.py:76
  242.5 23.3 %fusion.8 = f32[128,128,384]{0,1,2:T(8,128)} fusion(bf16[384,128,128]{2,1,0:T(8,128)(2,1)} %all-gather.5.cloned.1.call-done, bf16[384,64,64]{2,1,0:T(8,128)(2,1)} %get-tuple-element.15, bf16[384,64,64]{2,1,0:T(8,128)(2,1)} %get-tuple-element.14, bf16[384,64,128]{2,1,0:T(8,128)(2,1)} %all-gather.3.cloned.1.call-done), kind=kOutput, calls=%fused_computation.12 | convolution fusion | flops 1648361472 | bytes 50331648 | tf_op jit(solution)/shard_map/fiw,fjw->ijf/dot_general | solution.py:88
  265.8 14.7 %fusion = (bf16[128,64,384]{0,1,2:T(8,128)(2,1)}, bf16[128,64,384]{0,1,2:T(8,128)(2,1)}) fusion(f32[128,128,384]{0,1,2:T(8,128)} %fusion.8, f32[128,64]{0,1:T(8,128)S(1)} %fusion.20), kind=kLoop, calls=%fused_computation.3 | loop fusion | flops 12582912 | bytes 37781504 | tf_op jit(solution)/shard_map/convert_element_type | solution.py:90
  280.5 9.7 %copy.29 = bf16[128,64,384]{2,1,0:T(8,128)(2,1)} copy(bf16[128,64,384]{0,1,2:T(8,128)(2,1)} %get-tuple-element.13) | data formatting | bytes 12582912
  290.2 9.7 %copy.30 = bf16[128,64,384]{2,1,0:T(8,128)(2,1)} copy(bf16[128,64,384]{0,1,2:T(8,128)(2,1)} %get-tuple-element.12) | data formatting | bytes 12582912
  (14 shorter events, 0.1 us)
Async XLA Ops:
  9.6 31.5 %all-to-all-start = ((bf16[16,1,2]{2,1,0:T(2,128)(2,1)}), bf16[16,1,2]{2,1,0:T(2,128)(2,1)S(1)}, u32[]{:S(2)}, u32[]{:S(2)}) async-start(bf16[16,1,2]{2,1,0:T(2,128)(2,1)} %convert_element_type.74), calls=%async_computation | async-start | bytes 16384 | tf_op jit(solution)/shard_map/all_to_all | solution.py:65
  41.1 7.4 %copy-start = (s32[8,64]{1,0:T(8,128)S(1)}, s32[8,64]{1,0:T(8,128)}, u32[]{:S(2)}) copy-start(s32[8,64]{1,0:T(8,128)} %param.7) | copy-start | bytes 6148
  41.1 50.0 %all-to-all-start.1 = ((bf16[16,2,64,768]{3,2,1,0:T(8,128)(2,1)}), bf16[16,2,64,768]{3,2,1,0:T(8,128)(2,1)S(1)}, u32[]{:S(2)}, u32[]{:S(2)}) async-start(bf16[16,2,64,768]{3,2,1,0:T(8,128)(2,1)} %broadcast_select_fusion), calls=%async_computation.1 | async-start | bytes 6291456 | tf_op jit(solution)/shard_map/all_to_all | solution.py:64
  48.5 92.8 %all-gather.3.cloned.1.call-start = ((), (), s32[]{:S(2)}) async-start(), calls=%async_computation.2 | async-start | bytes 7077888 | tf_op jit(solution)/shard_map/all_gather | solution.py:80
  97.2 145.3 %all-gather.5.cloned.1.call-start = ((), (), s32[]{:S(2)}) async-start(), calls=%async_computation.3 | async-start | bytes 13369344 | tf_op jit(solution)/shard_map/all_gather | solution.py:76
Sparse Core Ops, SparseCore 0:
  97.3 43.9 all-gather.2
  143.4 99.0 all-gather.4

commit v2 on v1

--- a/solution.py
+++ b/solution.py
@@ -59,35 +59,39 @@
     labels = local_id.astype(jnp.bfloat16).reshape(columns, CAP)
     table = transform_table()
     local_white = whiten(recorded, table)
-    payload = jnp.take(local_white, source, axis=0).reshape(columns, CAP, W, 2 * F)
-    arrived, tags = (
-        lax.all_to_all(payload, "col", split_axis=0, concat_axis=0, tiled=True),
-        lax.all_to_all(labels, "col", split_axis=0, concat_axis=0, tiled=True),
-    )
-    tags = tags.reshape(outgoing).astype(jnp.int32)
-    flat = arrived.reshape(outgoing, W, arrived.shape[3])
+    payload = jnp.take(local_white, source, axis=0).reshape(columns, CAP * W, 2 * F)
+    label_rows = jnp.zeros((columns, 8, 2 * F), jnp.bfloat16).at[:, 0, :CAP].set(labels)
+    payload = jnp.concatenate([payload, label_rows], axis=1)
+    arrived = lax.all_to_all(payload, "col", split_axis=0, concat_axis=0, tiled=True)
+    tags = arrived[:, CAP * W, :CAP].reshape(outgoing).astype(jnp.int32)
+    flat = arrived[:, : CAP * W, :].reshape(outgoing, W, 2 * F)
     match = tags[None, :] == jnp.arange(owned, dtype=jnp.int32)[:, None]
     pick = jnp.sum(jnp.where(match, jnp.arange(outgoing, dtype=jnp.int32)[None, :], 0), axis=1)
     spectra = jnp.take(flat, pick, axis=0)
     mask_float = window_mask.astype(jnp.bfloat16)
     spectra = spectra * mask_float[:, :, None]
     stacked = spectra.reshape(owned, W, 2, F).transpose(3, 0, 2, 1).reshape(F, owned, 2 * W)
-    left, left_mask = (
-        lax.all_gather(stacked, "col", axis=1, tiled=True),
-        lax.all_gather(mask_float, "col", axis=0, tiled=True),
-    )
-    right, right_mask = (
-        lax.all_gather(stacked, "row", axis=1, tiled=True),
-        lax.all_gather(mask_float, "row", axis=0, tiled=True),
-    )
+    mask_row = jnp.concatenate([mask_float, jnp.zeros_like(mask_float)], axis=1)
+    stacked = jnp.concatenate([stacked, mask_row[None]], axis=0)
+    left_all = lax.all_gather(stacked, "col", axis=1, tiled=True)
+    right_all = lax.all_gather(stacked, "row", axis=1, tiled=True)
+    left, left_mask = left_all[:F], left_all[F, :, :W]
+    right, right_mask = right_all[:F], right_all[F, :, :W]
     counts = jnp.dot(left_mask, right_mask.T, preferred_element_type=jnp.float32)
     inverse = 1.0 / jnp.maximum(counts, 1.0)
-    across = right.shape[1]
-    turned = jnp.concatenate([right[:, :, W:], -right[:, :, :W]], axis=2)
-    both = jnp.concatenate([right, turned], axis=1)
-    product = jnp.einsum("fiw,fjw->ijf", left, both, preferred_element_type=jnp.float32)
-    real_part = (product[:, :across, :] * inverse[:, :, None]).astype(jnp.bfloat16)
-    imag_part = (product[:, across:, :] * inverse[:, :, None]).astype(jnp.bfloat16)
+    lane = jnp.arange(2 * W, dtype=jnp.int32)
+    swap = jnp.where(
+        lane[:, None] == (lane[None, :] + W) % (2 * W),
+        jnp.where(lane[None, :] < W, 1.0, -1.0),
+        0.0,
+    ).astype(jnp.bfloat16)
+    turned = jnp.einsum("fjw,wv->fjv", right, swap, preferred_element_type=jnp.float32).astype(
+        jnp.bfloat16
+    )
+    real = jnp.einsum("fiw,fjw->ijf", left, right, preferred_element_type=jnp.float32)
+    imag = jnp.einsum("fiw,fjw->ijf", left, turned, preferred_element_type=jnp.float32)
+    real_part = (real * inverse[:, :, None]).astype(jnp.bfloat16)
+    imag_part = (imag * inverse[:, :, None]).astype(jnp.bfloat16)
     return (real_part, imag_part)
 
 

time: 308 us -> 306 us (level)
  waiting for transfers between devices: 142 us -> 182 us
  blocking collectives: 33.9 us -> 0 us
  other arithmetic: 40.3 us -> 16 us
  matrix products: 30.8 us -> 42.7 us
  local copies, waits for them, and re-layouts: 30.6 us -> 41.2 us
  starting transfers between devices: 14.6 us -> 7.56 us
    all_gather x2, waiting for transfers between devices: 98.6 us -> 137 us  [the longest x1 101 us: per_device(): left_all = lax.all_gather(stacked, 'col', axis=1, tiled=True)]
    all_gather x2 -> x0, blocking collectives: 33.9 us -> none  [the longest x1 21.1 us: per_device(): lax.all_gather(mask_float, 'col', axis=0, tiled=True)]
    convert_element_type x2 -> x1, other arithmetic: 14.7 us -> 0.03 us  [per_device(): tags = arrived[:, CAP * W, :CAP].reshape(outgoing).astype(jnp.int32)]
    slice x1 -> x0, other arithmetic: 11.9 us -> none  [per_device(): turned = jnp.concatenate([right[:, :, W:], -right[:, :, :W]], axis=2)]
    dot_general x1 -> x2, matrix products: 23.3 us -> 34.5 us  [the longest x1 20.4 us: per_device(): jnp.einsum('fiw,fjw->ijf', left, right, preferred_element_type=jnp.float32)]
    dot_general x0 -> x1, local copies, waits for them, and re-layouts: none -> 10.7 us  [per_device(): jnp.einsum('fiw,fjw->ijf', left, right, preferred_element_type=jnp.float32)]
    all_to_all x1 -> x0, starting transfers between devices: 7.15 us -> none  [per_device(): lax.all_to_all(labels, 'col', split_axis=0, concat_axis=0, tiled=True)]
    unnamed x4 -> x8, local copies, waits for them, and re-layouts: 19.4 us -> 19.4 us
  transfers between devices with their start and end apart: 4 -> 3, of which waited for: 3 -> 3; matrix products, arithmetic and copies ran while one was open for 12% -> 4% of each run, Pallas kernels for 0% -> 0%
where the time goes in v2:
time: 306 us; the launch traced here: 304 us
  waiting for transfers between devices  182 us (59%)
  matrix products  42.7 us (14%)
  local copies, waits for them, and re-layouts  41.2 us (13%)
  other arithmetic  16 us (5%)
  between operations  14.9 us (5%)
  starting transfers between devices  7.56 us (2%)
    all_gather x1, waiting for transfers between devices, per_device(): left_all = lax.all_gather(stacked, 'col', axis=1, tiled=True)  101 us
    all_to_all x1, waiting for transfers between devices, per_device(): lax.all_to_all(payload, 'col', split_axis=0, concat_axis=0, tiled=True)  44.6 us
    all_gather x1, waiting for transfers between devices, per_device(): right_all = lax.all_gather(stacked, 'row', axis=1, tiled=True)  35.7 us
    dot_general x1, matrix products, per_device(): jnp.einsum('fiw,fjw->ijf', left, right, preferred_element_type=jnp.float32)  20.4 us
    unnamed x8, local copies, waits for them, and re-layouts  19.4 us
    dot_general x1, matrix products, per_device(): jnp.einsum('fiw,fjw->ijf', left, turned, preferred_element_type=jnp.float32)  14.1 us
    dot_general x1, local copies, waits for them, and re-layouts, per_device(): jnp.einsum('fiw,fjw->ijf', left, right, preferred_element_type=jnp.float32)  10.7 us
    all_to_all x1, starting transfers between devices, per_device(): lax.all_to_all(payload, 'col', split_axis=0, concat_axis=0, tiled=True)  7.3 us
  transfers between devices with their start and end apart: 3, of which 3 were waited for; matrix products, arithmetic and copies ran while one was open for 4% of the time, Pallas kernels for 0%

profile of v2, /device:TPU:0, one launch (start us, length us, event | category | flops | bytes accessed | tf_op | source)
XLA Modules:
  0.0 304.2 jit_solution(10234694158219215910)
XLA Ops:
  7.8 0.7 fusion.52
  8.5 0.1 fusion.51
  8.6 0.2 select_reduce_fusion.2
  8.8 0.1 select_reduce_fusion.1
  8.9 0.1 reduce_sum.53
  9.0 0.1 broadcast_in_dim.113
  9.1 0.1 broadcast_in_dim.114
  9.2 0.1 convert_element_type.82
  9.3 0.4 fusion.32
  9.7 0.4 fusion.39
  10.1 2.0 subtract_convert_fusion
  12.1 7.3 %fusion.21 = f32[1024,768]{0,1:T(8,128)S(1)} fusion(bf16[1024,3072]{1,0:T(8,128)(2,1)} %bitcast.67, bf16[3072,384]{1,0:T(8,128)(2,1)S(1)} %bitcast.66, bf16[3072,384]{1,0:T(8,128)(2,1)S(1)} %bitcast.65), kind=kOutput, calls=%fused_computation.24 | convolution fusion | flops 4841275392 | bytes 14155776 | tf_op jit(solution)/shard_map/dot_general | solution.py:32
  19.4 1.5 multiply_add_fusion
  20.9 1.6 reduce_sum.54
  22.5 1.6 fusion.24
  24.0 1.5 copy.23
  25.5 1.5 copy.24
  27.0 0.2 pad_maximum_fusion
  27.2 2.4 gather_fusion
  29.6 2.1 bitcast_select_fusion
  31.7 2.0 fusion.16
  33.7 7.3 %all-to-all-start = ((bf16[16,136,768]{2,1,0:T(8,128)(2,1)}), bf16[16,136,768]{2,1,0:T(8,128)(2,1)S(1)}, u32[]{:S(2)}, u32[]{:S(2)}) async-start(bf16[16,136,768]{2,1,0:T(8,128)(2,1)} %fusion.16), calls=%async_computation | async-start | bytes 6684672 | tf_op jit(solution)/shard_map/all_to_all | solution.py:65
  41.0 0.0 all-gather.5.cloned.1.call-start
  41.0 0.0 copy-done
  41.1 44.6 %all-to-all-done = bf16[16,136,768]{2,1,0:T(8,128)(2,1)S(1)} async-done(((bf16[16,136,768]{2,1,0:T(8,128)(2,1)}), bf16[16,136,768]{2,1,0:T(8,128)(2,1)S(1)}, u32[]{:S(2)}, u32[]{:S(2)}) %all-to-all-start) | async-done | bytes 3342368 | tf_op jit(solution)/shard_map/all_to_all | solution.py:65
  85.7 0.1 reshape.307
  85.8 0.1 select_reduce_fusion.3
  86.0 2.0 slice.62
  87.9 2.5 gather_fusion.1
  90.4 0.2 gather.15
  90.6 1.0 multiply_bitcast_fusion
  91.7 0.1 copy.26
  91.8 0.5 copy.27
  92.3 0.9 pad_maximum_fusion.1
  93.3 0.0 all-gather.5.cloned.1.call-update
  93.3 0.2 all-gather.3.cloned.1.call-start
  93.5 0.5 all-gather.3.cloned.1.call-update
  94.1 0.6 and_select_fusion
  94.6 0.5 compare_select_fusion.8
  95.1 101.0 %all-gather.5.cloned.1.call-done = bf16[385,128,128]{2,1,0:T(8,128)(2,1)} async-done(((bf16[385,8,128]{2,1,0:T(8,128)(2,1)}), bf16[385,128,128]{2,1,0:T(8,128)(2,1)}) %all-gather.5.cloned.1.call-update) | async-done | bytes 12615696 | tf_op jit(solution)/shard_map/all_gather | solution.py:76
  196.1 10.7 %fusion.66 = bf16[384,128,128]{2,1,0:T(8,128)(2,1)} fusion(bf16[385,128,128]{2,1,0:T(8,128)(2,1)} %all-gather.5.cloned.1.call-done), kind=kLoop, calls=%fused_computation.9.clone.clone.clone.1 | loop fusion | bytes 25165824 | tf_op jit(solution)/shard_map/fiw,fjw->ijf/dot_general | solution.py:91
  206.9 35.7 %all-gather.3.cloned.1.call-done = bf16[385,64,128]{2,1,0:T(8,128)(2,1)} async-done(((bf16[385,8,128]{2,1,0:T(8,128)(2,1)}), bf16[385,64,128]{2,1,0:T(8,128)(2,1)}) %all-gather.3.cloned.1.call-update) | async-done | bytes 6307856 | tf_op jit(solution)/shard_map/all_gather | solution.py:77
  242.5 0.9 fusion.26
  243.4 20.4 %fusion.1 = bf16[128,64,384]{0,1,2:T(8,128)(2,1)} fusion(f32[128,64]{0,1:T(8,128)S(1)} %fusion.26, bf16[385,64,128]{2,1,0:T(8,128)(2,1)} %all-gather.3.cloned.1.call-done, bf16[384,128,128]{2,1,0:T(8,128)(2,1)} %fusion.66), kind=kOutput, calls=%fused_computation.5 | convolution fusion | flops 811597824 | bytes 25214976 | tf_op jit(solution)/shard_map/fiw,fjw->ijf/dot_general | solution.py:91
  263.9 9.7 %copy.28 = bf16[128,64,384]{2,1,0:T(8,128)(2,1)} copy(bf16[128,64,384]{0,1,2:T(8,128)(2,1)} %fusion.1) | data formatting | bytes 12582912
  273.6 0.0 copy-done.1
  273.6 14.1 %fusion = bf16[128,64,384]{0,1,2:T(8,128)(2,1)} fusion(f32[128,64]{0,1:T(8,128)S(1)} %fusion.26, bf16[385,128,128]{2,1,0:T(8,128)(2,1)} %all-gather.5.cloned.1.call-done, bf16[385,64,128]{2,1,0:T(8,128)(2,1)} %all-gather.3.cloned.1.call-done, bf16[128]{0:T(256)(128)(2,1)S(1)} %copy-done.2, s32[128]{0:T(128)S(1)} %copy-done.1), kind=kOutput, calls=%fused_computation.3 | convolution fusion | flops 1620082688 | bytes 25215744 | tf_op jit(solution)/shard_map/fiw,fjw->ijf/dot_general | solution.py:92
  287.6 9.7 %copy.29 = bf16[128,64,384]{2,1,0:T(8,128)(2,1)} copy(bf16[128,64,384]{0,1,2:T(8,128)(2,1)} %fusion) | data formatting | bytes 12582912
  (19 shorter events, 0.2 us)
Async XLA Ops:
  33.7 7.4 %copy-start = (s32[8,64]{1,0:T(8,128)S(1)}, s32[8,64]{1,0:T(8,128)}, u32[]{:S(2)}) copy-start(s32[8,64]{1,0:T(8,128)} %param.9) | copy-start | bytes 6148
  33.7 52.0 %all-to-all-start = ((bf16[16,136,768]{2,1,0:T(8,128)(2,1)}), bf16[16,136,768]{2,1,0:T(8,128)(2,1)S(1)}, u32[]{:S(2)}, u32[]{:S(2)}) async-start(bf16[16,136,768]{2,1,0:T(8,128)(2,1)} %fusion.16), calls=%async_computation | async-start | bytes 6684672 | tf_op jit(solution)/shard_map/all_to_all | solution.py:65
  41.0 155.1 %all-gather.5.cloned.1.call-start = ((), (), s32[]{:S(2)}) async-start(), calls=%async_computation.2 | async-start | bytes 13404160 | tf_op jit(solution)/shard_map/all_gather | solution.py:76
  93.3 149.2 %all-gather.3.cloned.1.call-start = ((), (), s32[]{:S(2)}) async-start(), calls=%async_computation.1 | async-start | bytes 7096320 | tf_op jit(solution)/shard_map/all_gather | solution.py:77
  263.9 9.7 %copy-start.1 = (s32[128]{0:T(128)S(1)}, s32[128]{0:T(128)}, u32[]{:S(2)}) copy-start(s32[128]{0:T(128)} %and_select_fusion) | copy-start | bytes 1540
  263.9 9.7 %copy-start.2 = (bf16[128]{0:T(256)(128)(2,1)S(1)}, bf16[128]{0:T(256)(128)(2,1)}, u32[]{:S(2)}) copy-start(bf16[128]{0:T(256)(128)(2,1)} %compare_select_fusion.8) | copy-start | bytes 772
Sparse Core Ops, SparseCore 0:
  93.4 102.6 all-gather.4
  198.4 44.0 all-gather.2

commit v3 on v2

v3 whole, which is shorter than its diff:
```python
import math

import jax
import jax.numpy as jnp
from jax import lax
from jax.sharding import PartitionSpec as P

F = 384
L = 3072
F0 = 13
BAND = 64
CAP = 2
CHUNKS = 3
W = 64


def transform_table(first, count):
    freqs = jnp.arange(count, dtype=jnp.int32) + (F0 + first)
    high = jnp.arange(L // 64, dtype=jnp.int32)[:, None] * 64 * freqs[None, :] % L
    low = jnp.arange(64, dtype=jnp.int32)[:, None] * freqs[None, :] % L
    scale = 2.0 * math.pi / L
    ah = high.astype(jnp.float32) * scale
    al = low.astype(jnp.float32) * scale
    ch, sh = jnp.cos(ah)[:, None, :], jnp.sin(ah)[:, None, :]
    cl, sl = jnp.cos(al)[None, :, :], jnp.sin(al)[None, :, :]
    cos_part = (ch * cl - sh * sl).reshape(L, count)
    sin_part = (sh * cl + ch * sl).reshape(L, count)
    return jnp.concatenate([cos_part, -sin_part], axis=1).astype(jnp.bfloat16)


def whiten(segments, table):
    count = segments.shape[0]
    width = table.shape[1] // 2
    spectrum = jnp.dot(segments.reshape(count * W, L), table, preferred_element_type=jnp.float32)
    real = spectrum[:, :width]
    imag = spectrum[:, width:]
    power = (real * real + imag * imag).reshape(count * W, width // BAND, BAND)
    factor = lax.rsqrt(jnp.mean(power, axis=2) + 1e-05)
    factor = jnp.repeat(factor, BAND, axis=1)
    white = jnp.concatenate([real * factor, imag * factor], axis=1)
    return white.astype(jnp.bfloat16).reshape(count, W, 2 * width)


def per_device(recorded, seg_count, slot_station, window_mask):
    columns = lax.axis_size("col")
    slots_here = recorded.shape[0]
    owned = window_mask.shape[0]
    outgoing = columns * CAP
    slot_index = jnp.arange(slots_here, dtype=jnp.int32)
    live = slot_index < seg_count[0]
    target_col = jnp.where(live, slot_station // owned % columns, columns)
    onehot = (target_col[:, None] == jnp.arange(columns, dtype=jnp.int32)[None, :]).astype(
        jnp.int32
    )
    earlier = jnp.cumsum(onehot, axis=0) - onehot
    rank = jnp.sum(earlier * onehot, axis=1)
    position = jnp.where(live, target_col * CAP + rank, outgoing)
    chosen = position[None, :] == jnp.arange(outgoing, dtype=jnp.int32)[:, None]
    source = jnp.sum(jnp.where(chosen, slot_index[None, :], 0), axis=1)
    local_id = jnp.sum(jnp.where(chosen, slot_station[None, :] % owned + 1, 0), axis=1) - 1
    labels = local_id.astype(jnp.bfloat16).reshape(columns, CAP)
    mask_float = window_mask.astype(jnp.bfloat16)
    lane = jnp.arange(2 * W, dtype=jnp.int32)
    swap = jnp.where(
        lane[:, None] == (lane[None, :] + W) % (2 * W),
        jnp.where(lane[None, :] < W, 1.0, -1.0),
        0.0,
    ).astype(jnp.bfloat16)
    chunk = F // CHUNKS
    pick = inverse = None
    reals, imags = [], []
    for k in range(CHUNKS):
        table = transform_table(k * chunk, chunk)
        local_white = whiten(recorded, table)
        payload = jnp.take(local_white, source, axis=0).reshape(columns, CAP * W, 2 * chunk)
        if k == 0:
            label_rows = jnp.zeros((columns, 8, 2 * chunk), jnp.bfloat16).at[:, 0, :CAP].set(labels)
            payload = jnp.concatenate([payload, label_rows], axis=1)
        arrived = lax.all_to_all(payload, "col", split_axis=0, concat_axis=0, tiled=True)
        if k == 0:
            tags = arrived[:, CAP * W, :CAP].reshape(outgoing).astype(jnp.int32)
            match = tags[None, :] == jnp.arange(owned, dtype=jnp.int32)[:, None]
            pick = jnp.sum(
                jnp.where(match, jnp.arange(outgoing, dtype=jnp.int32)[None, :], 0), axis=1
            )
        flat = arrived[:, : CAP * W, :].reshape(outgoing, W, 2 * chunk)
        spectra = jnp.take(flat, pick, axis=0) * mask_float[:, :, None]
        stacked = spectra.reshape(owned, W, 2, chunk).transpose(3, 0, 2, 1)
        stacked = stacked.reshape(chunk, owned, 2 * W)
        if k == 0:
            mask_row = jnp.concatenate([mask_float, jnp.zeros_like(mask_float)], axis=1)
            stacked = jnp.concatenate([stacked, mask_row[None]], axis=0)
        left = lax.all_gather(stacked, "col", axis=1, tiled=True)
        right = lax.all_gather(stacked, "row", axis=1, tiled=True)
        if k == 0:
            left_mask, right_mask = left[chunk, :, :W], right[chunk, :, :W]
            left, right = left[:chunk], right[:chunk]
            counts = jnp.dot(left_mask, right_mask.T, preferred_element_type=jnp.float32)
            inverse = 1.0 / jnp.maximum(counts, 1.0)
        turned = jnp.einsum(
            "fjw,wv->fjv", right, swap, preferred_element_type=jnp.float32
        ).astype(jnp.bfloat16)
        real = jnp.einsum("fiw,fjw->ijf", left, right, preferred_element_type=jnp.float32)
        imag = jnp.einsum("fiw,fjw->ijf", left, turned, preferred_element_type=jnp.float32)
        reals.append((real * inverse[:, :, None]).astype(jnp.bfloat16))
        imags.append((imag * inverse[:, :, None]).astype(jnp.bfloat16))
    return (jnp.concatenate(reals, axis=2), jnp.concatenate(imags, axis=2))


def solution(mesh):
    placed = (
        P(("row", "col"), None, None),
        P(("row", "col")),
        P(("row", "col")),
        P(("row", "col"), None),
    )
    return jax.shard_map(
        per_device,
        mesh=mesh,
        in_specs=placed,
        out_specs=(P("row", "col", None), P("row", "col", None)),
        check_vma=False,
    )
```

time: 306 us -> 427 us (1.40)
  waiting for transfers between devices: 182 us -> 272 us
  blocking collectives: 0 us -> 19.5 us
  matrix products: 42.7 us -> 53 us
  local copies, waits for them, and re-layouts: 41.2 us -> 32.3 us
  other arithmetic: 16 us -> 21.6 us
    all_gather x2 -> x6, waiting for transfers between devices: 137 us -> 240 us  [the longest x3 171 us: per_device(): left = lax.all_gather(stacked, 'col', axis=1, tiled=True)]
    all_to_all x0 -> x1, blocking collectives: none -> 19.5 us  [per_device(): lax.all_to_all(payload, 'col', split_axis=0, concat_axis=0, tiled=True)]
    all_to_all x1 -> x2, waiting for transfers between devices: 44.6 us -> 31.2 us  [per_device(): lax.all_to_all(payload, 'col', split_axis=0, concat_axis=0, tiled=True)]
    concatenate x0 -> x2, other arithmetic: none -> 11.8 us  [per_device(): return (jnp.concatenate(reals, axis=2), jnp.concatenate(imags, axis=2))]
    dot_general x1 -> x3, matrix products: 7.29 us -> 14 us  [whiten(): jnp.dot(segments.reshape(count * W, L), table, preferred_element_type=jnp...]
    dot_general x1 -> x3, matrix products: 14.1 us -> 20.7 us  [per_device(): jnp.einsum('fiw,fjw->ijf', left, turned, preferred_element_type=jnp.float32)]
    dot_general x1, local copies, waits for them, and re-layouts: 10.7 us -> 4.79 us  [per_device(): jnp.einsum('fiw,fjw->ijf', left, right, preferred_element_type=jnp.float32)]
    all_to_all x1 -> x2, starting transfers between devices: 7.3 us -> 10.9 us  [per_device(): lax.all_to_all(payload, 'col', split_axis=0, concat_axis=0, tiled=True)]
  transfers between devices with their start and end apart: 3 -> 8, of which waited for: 3 -> 8; matrix products, arithmetic and copies ran while one was open for 4% -> 5% of each run, Pallas kernels for 0% -> 0%
where the time goes in v3:
time: 427 us; the launch traced here: 425 us
  waiting for transfers between devices  272 us (64%)
  matrix products  53 us (12%)
  local copies, waits for them, and re-layouts  32.3 us (8%)
  other arithmetic  21.6 us (5%)
  blocking collectives  19.5 us (5%)
  between operations  15.2 us (4%)
  starting transfers between devices  11.4 us (3%)
    all_gather x3, waiting for transfers between devices, per_device(): left = lax.all_gather(stacked, 'col', axis=1, tiled=True)  171 us
    all_gather x3, waiting for transfers between devices, per_device(): right = lax.all_gather(stacked, 'row', axis=1, tiled=True)  69 us
    all_to_all x2, waiting for transfers between devices, per_device(): lax.all_to_all(payload, 'col', split_axis=0, concat_axis=0, tiled=True)  31.2 us
    dot_general x3, matrix products, per_device(): jnp.einsum('fiw,fjw->ijf', left, turned, preferred_element_type=jnp.float32)  20.7 us
    all_to_all x1, blocking collectives, per_device(): lax.all_to_all(payload, 'col', split_axis=0, concat_axis=0, tiled=True)  19.5 us
    unnamed x14, local copies, waits for them, and re-layouts  19.4 us
    dot_general x3, matrix products, per_device(): jnp.einsum('fiw,fjw->ijf', left, right, preferred_element_type=jnp.float32)  17.4 us
    dot_general x3, matrix products, whiten(): jnp.dot(segments.reshape(count * W, L), table, preferred_element_type=jnp...  14 us
  transfers between devices with their start and end apart: 8, of which 8 were waited for; matrix products, arithmetic and copies ran while one was open for 5% of the time, Pallas kernels for 0%

profile of v3, /device:TPU:0, one launch (start us, length us, event | category | flops | bytes accessed | tf_op | source)
XLA Modules:
  0.0 425.4 jit_solution(2234569262803397218)
XLA Ops:
  7.9 0.7 compare_select_fusion.11
  8.6 0.2 select_reduce_fusion.2
  9.4 1.0 fusion.114
  10.4 0.5 subtract_convert_fusion.2
  10.9 4.7 %fusion.44 = f32[1024,256]{0,1:T(8,128)S(1)} fusion(bf16[1024,3072]{1,0:T(8,128)(2,1)} %bitcast.140, bf16[3072,128]{1,0:T(8,128)(2,1)S(1)} %bitcast.135, bf16[3072,128]{1,0:T(8,128)(2,1)S(1)} %bitcast.134), kind=kOutput, calls=%fused_computation.52 | convolution fusion | flops 1613758464 | bytes 8912896 | tf_op jit(solution)/shard_map/dot_general | solution.py:34
  16.0 0.2 copy.26
  16.2 1.7 subtract_convert_fusion
  17.9 4.7 %fusion.41 = f32[1024,256]{0,1:T(8,128)S(1)} fusion(bf16[1024,3072]{1,0:T(8,128)(2,1)} %bitcast.141, bf16[3072,128]{1,0:T(8,128)(2,1)S(1)} %bitcast.138, bf16[3072,128]{1,0:T(8,128)(2,1)S(1)} %bitcast.139), kind=kOutput, calls=%fused_computation.51 | convolution fusion | flops 1613758464 | bytes 8912896 | tf_op jit(solution)/shard_map/dot_general | solution.py:34
  23.0 4.6 %fusion.38 = f32[1024,256]{0,1:T(8,128)S(1)} fusion(bf16[1024,3072]{1,0:T(8,128)(2,1)} %bitcast.142, bf16[3072,128]{1,0:T(8,128)(2,1)S(1)} %bitcast.137, bf16[3072,128]{1,0:T(8,128)(2,1)S(1)} %bitcast.136), kind=kOutput, calls=%fused_computation.50 | convolution fusion | flops 1613758464 | bytes 8912896 | tf_op jit(solution)/shard_map/dot_general | solution.py:34
  28.0 0.2 copy.36
  28.4 0.6 gather_fusion
  29.1 0.6 gather_fusion.2
  29.8 1.6 gather_fusion.4
  31.4 3.1 broadcast_select_fusion.1
  34.5 7.3 %all-to-all-start.2 = ((bf16[16,128,256]{2,1,0:T(8,128)(2,1)}), bf16[16,128,256]{2,1,0:T(8,128)(2,1)S(1)}, u32[]{:S(2)}, u32[]{:S(2)}) async-start(bf16[16,128,256]{2,1,0:T(8,128)(2,1)} %bitcast.117), calls=%async_computation.2 | async-start | bytes 2097152 | tf_op jit(solution)/shard_map/all_to_all | solution.py:79
  42.0 17.5 %all-to-all-done.2 = bf16[16,128,256]{2,1,0:T(8,128)(2,1)S(1)} async-done(((bf16[16,128,256]{2,1,0:T(8,128)(2,1)}), bf16[16,128,256]{2,1,0:T(8,128)(2,1)S(1)}, u32[]{:S(2)}, u32[]{:S(2)}) %all-to-all-start.2) | async-done | bytes 1048608 | tf_op jit(solution)/shard_map/all_to_all | solution.py:79
  59.5 19.5 %all_to_all.15 = bf16[16,136,256]{2,1,0:T(8,128)(2,1)S(1)} all-to-all(bf16[16,136,256]{2,1,0:T(8,128)(2,1)S(1)} %fusion.47), channel_id=1, replica_groups=mesh['row'=8,'col'=16] {'col'}, dimensions={0} | all-to-all | bytes 2228224 | tf_op jit(solution)/shard_map/all_to_all | solution.py:79
  79.0 3.7 all-to-all-start.1
  83.0 0.6 gather_fusion.5
  83.6 13.6 %all-to-all-done.1 = bf16[16,128,256]{2,1,0:T(8,128)(2,1)S(1)} async-done(((bf16[16,128,256]{2,1,0:T(8,128)(2,1)}), bf16[16,128,256]{2,1,0:T(8,128)(2,1)S(1)}, u32[]{:S(2)}, u32[]{:S(2)}) %all-to-all-start.1) | async-done | bytes 1048608 | tf_op jit(solution)/shard_map/all_to_all | solution.py:79
  97.2 0.6 gather_fusion.3
  97.9 0.6 gather_fusion.1
  98.7 0.2 copy.29
  98.9 0.7 pad_maximum_fusion.5
  99.7 0.2 all-gather.7.cloned.1.call-start
  99.9 0.5 all-gather.7.cloned.1.call-update
  100.6 0.9 copy.33
  101.6 0.5 all-gather.13.cloned.1.call-update
  102.3 0.9 copy.38
  103.2 0.5 all-gather.17.cloned.1.call-update
  103.8 51.8 %all-gather.9.cloned.1.call-done = bf16[129,128,128]{2,1,0:T(8,128)(2,1)} async-done(((bf16[129,8,128]{2,1,0:T(8,128)(2,1)}), bf16[129,128,128]{2,1,0:T(8,128)(2,1)}) %all-gather.9.cloned.1.call-update) | async-done | bytes 4227088 | tf_op jit(solution)/shard_map/all_gather | solution.py:93
  155.6 4.8 %fusion.152 = bf16[128,128,128]{2,1,0:T(8,128)(2,1)} fusion(bf16[129,128,128]{2,1,0:T(8,128)(2,1)} %all-gather.9.cloned.1.call-done), kind=kLoop, calls=%fused_computation.23.clone.clone.clone.1 | loop fusion | bytes 8388608 | tf_op jit(solution)/shard_map/fiw,fjw->ijf/dot_general | solution.py:103
  160.4 24.0 %all-gather.7.cloned.1.call-done = bf16[129,64,128]{2,1,0:T(8,128)(2,1)} async-done(((bf16[129,8,128]{2,1,0:T(8,128)(2,1)}), bf16[129,64,128]{2,1,0:T(8,128)(2,1)}) %all-gather.7.cloned.1.call-update) | async-done | bytes 2113552 | tf_op jit(solution)/shard_map/all_gather | solution.py:94
  184.3 0.9 fusion.48
  185.2 28.6 %all-gather.11.cloned.1.call-done = bf16[128,64,128]{2,1,0:T(8,128)(2,1)} async-done(((bf16[128,8,128]{2,1,0:T(8,128)(2,1)}), bf16[128,64,128]{2,1,0:T(8,128)(2,1)}) %all-gather.11.cloned.1.call-update) | async-done | bytes 2097168 | tf_op jit(solution)/shard_map/all_gather | solution.py:94
  213.8 59.5 %all-gather.13.cloned.1.call-done = bf16[128,128,128]{2,1,0:T(8,128)(2,1)} async-done(((bf16[128,8,128]{2,1,0:T(8,128)(2,1)}), bf16[128,128,128]{2,1,0:T(8,128)(2,1)}) %all-gather.13.cloned.1.call-update) | async-done | bytes 4194320 | tf_op jit(solution)/shard_map/all_gather | solution.py:93
  273.3 7.3 %fusion.4 = bf16[128,64,128]{0,1,2:T(8,128)(2,1)} fusion(bf16[128,64,128]{2,1,0:T(8,128)(2,1)} %all-gather.11.cloned.1.call-done, bf16[128,128,128]{2,1,0:T(8,128)(2,1)} %all-gather.13.cloned.1.call-done, f32[128,64]{0,1:T(8,128)S(1)} %fusion.48), kind=kOutput, calls=%fused_computation.17 | convolution fusion | flops 270532608 | bytes 8421376 | tf_op jit(solution)/shard_map/fiw,fjw->ijf/dot_general | solution.py:103
  280.5 4.2 fusion.5
  284.8 16.5 %all-gather.15.cloned.1.call-done = bf16[128,64,128]{2,1,0:T(8,128)(2,1)} async-done(((bf16[128,8,128]{2,1,0:T(8,128)(2,1)}), bf16[128,64,128]{2,1,0:T(8,128)(2,1)}) %all-gather.15.cloned.1.call-update) | async-done | bytes 2097168 | tf_op jit(solution)/shard_map/all_gather | solution.py:94
  301.2 59.5 %all-gather.17.cloned.1.call-done = bf16[128,128,128]{2,1,0:T(8,128)(2,1)} async-done(((bf16[128,8,128]{2,1,0:T(8,128)(2,1)}), bf16[128,128,128]{2,1,0:T(8,128)(2,1)}) %all-gather.17.cloned.1.call-update) | async-done | bytes 4194320 | tf_op jit(solution)/shard_map/all_gather | solution.py:93
  360.7 5.9 %fusion.3 = bf16[128,64,128]{0,1,2:T(8,128)(2,1)S(1)} fusion(bf16[128,64,128]{2,1,0:T(8,128)(2,1)} %all-gather.15.cloned.1.call-done, bf16[128,128,128]{2,1,0:T(8,128)(2,1)} %all-gather.17.cloned.1.call-done, f32[128,64]{0,1:T(8,128)S(1)} %fusion.48), kind=kOutput, calls=%fused_computation.15 | convolution fusion | flops 270532608 | bytes 8421376 | tf_op jit(solution)/shard_map/fiw,fjw->ijf/dot_general | solution.py:103
  366.7 5.7 %pad_maximum_fusion = bf16[128,64,384]{0,1,2:T(8,128)(2,1)} fusion(bf16[128,64,128]{0,1,2:T(8,128)(2,1)S(1)} %fusion.3, bf16[128,64,128]{0,1,2:T(8,128)(2,1)S(1)} %copy-done.3, bf16[128,64,128]{0,1,2:T(8,128)(2,1)S(1)} %copy-done.2), kind=kLoop, calls=%fused_computation.6 | loop fusion | flops 6291456 | bytes 12582912 | tf_op jit(solution)/shard_map/concatenate | solution.py:107
  372.3 9.7 %copy.40 = bf16[128,64,384]{2,1,0:T(8,128)(2,1)} copy(bf16[128,64,384]{0,1,2:T(8,128)(2,1)} %pad_maximum_fusion) | data formatting | bytes 12582912
  382.0 7.1 %fusion.1 = bf16[128,64,128]{0,1,2:T(8,128)(2,1)} fusion(bf16[128,128,128]{2,1,0:T(8,128)(2,1)} %all-gather.13.cloned.1.call-done, bf16[128,64,128]{2,1,0:T(8,128)(2,1)} %all-gather.11.cloned.1.call-done, f32[128,64]{0,1:T(8,128)S(1)} %fusion.48, bf16[128]{0:T(256)(128)(2,1)S(1)} %compare_select_fusion.6, s32[128]{0:T(128)S(1)} %and_select_fusion), kind=kOutput, calls=%fused_computation.11 | convolution fusion | flops 540049408 | bytes 8422144 | tf_op jit(solution)/shard_map/fiw,fjw->ijf/dot_general | solution.py:104
  389.1 7.1 %fusion = bf16[128,64,128]{0,1,2:T(8,128)(2,1)} fusion(bf16[128,128,128]{2,1,0:T(8,128)(2,1)} %all-gather.17.cloned.1.call-done, bf16[128,64,128]{2,1,0:T(8,128)(2,1)} %all-gather.15.cloned.1.call-done, f32[128,64]{0,1:T(8,128)S(1)} %fusion.48, bf16[128]{0:T(256)(128)(2,1)S(1)} %compare_select_fusion.6, s32[128]{0:T(128)S(1)} %and_select_fusion), kind=kOutput, calls=%fused_computation.9 | convolution fusion | flops 540049408 | bytes 8422144 | tf_op jit(solution)/shard_map/fiw,fjw->ijf/dot_general | solution.py:104
  396.2 6.5 %fusion.2 = bf16[128,64,128]{0,1,2:T(8,128)(2,1)} fusion(f32[128,64]{0,1:T(8,128)S(1)} %fusion.48, bf16[129,128,128]{2,1,0:T(8,128)(2,1)} %all-gather.9.cloned.1.call-done, bf16[129,64,128]{2,1,0:T(8,128)(2,1)S(1)} %copy-done, bf16[128]{0:T(256)(128)(2,1)S(1)} %compare_select_fusion.6, s32[128]{0:T(128)S(1)} %and_select_fusion), kind=kOutput, calls=%fused_computation.13 | convolution fusion | flops 540049408 | bytes 8438528 | tf_op jit(solution)/shard_map/fiw,fjw->ijf/dot_general | solution.py:104
  402.7 6.1 %pad_maximum_fusion.1 = bf16[128,64,384]{0,1,2:T(8,128)(2,1)} fusion(bf16[128,64,128]{0,1,2:T(8,128)(2,1)} %fusion, bf16[128,64,128]{0,1,2:T(8,128)(2,1)} %fusion.1, bf16[128,64,128]{0,1,2:T(8,128)(2,1)} %fusion.2), kind=kLoop, calls=%fused_computation.7 | loop fusion | flops 6291456 | bytes 12582912 | tf_op jit(solution)/shard_map/concatenate | solution.py:107
  408.9 9.7 %copy.41 = bf16[128,64,384]{2,1,0:T(8,128)(2,1)} copy(bf16[128,64,384]{0,1,2:T(8,128)(2,1)} %pad_maximum_fusion.1) | data formatting | bytes 12582912
  (70 shorter events, 3.5 us)
Async XLA Ops:
  34.5 7.4 %copy-start.4 = (bf16[32,64,256]{2,1,0:T(8,128)(2,1)S(1)}, bf16[32,64,256]{2,1,0:T(8,128)(2,1)}, u32[]{:S(2)}) copy-start(bf16[32,64,256]{2,1,0:T(8,128)(2,1)} %get-tuple-element.47) | copy-start | bytes 3145732
  34.5 25.0 %all-to-all-start.2 = ((bf16[16,128,256]{2,1,0:T(8,128)(2,1)}), bf16[16,128,256]{2,1,0:T(8,128)(2,1)S(1)}, u32[]{:S(2)}, u32[]{:S(2)}) async-start(bf16[16,128,256]{2,1,0:T(8,128)(2,1)} %bitcast.117), calls=%async_computation.2 | async-start | bytes 2097152 | tf_op jit(solution)/shard_map/all_to_all | solution.py:79
  42.0 40.7 %copy-start.5 = (s32[8,64]{1,0:T(8,128)S(1)}, s32[8,64]{1,0:T(8,128)}, u32[]{:S(2)}) copy-start(s32[8,64]{1,0:T(8,128)} %param.13) | copy-start | bytes 6148
  79.0 18.2 %all-to-all-start.1 = ((bf16[16,128,256]{2,1,0:T(8,128)(2,1)}), bf16[16,128,256]{2,1,0:T(8,128)(2,1)S(1)}, u32[]{:S(2)}, u32[]{:S(2)}) async-start(bf16[16,128,256]{2,1,0:T(8,128)(2,1)} %bitcast.24), calls=%async_computation.1 | async-start | bytes 2097152 | tf_op jit(solution)/shard_map/all_to_all | solution.py:79
  82.7 72.9 %all-gather.9.cloned.1.call-start = ((), (), s32[]{:S(2)}) async-start(), calls=%async_computation.4 | async-start | bytes 4491264 | tf_op jit(solution)/shard_map/all_gather | solution.py:93
  99.7 84.6 %all-gather.7.cloned.1.call-start = ((), (), s32[]{:S(2)}) async-start(), calls=%async_computation.3 | async-start | bytes 2377728 | tf_op jit(solution)/shard_map/all_gather | solution.py:94
  100.4 113.4 %all-gather.11.cloned.1.call-start = ((), (), s32[]{:S(2)}) async-start(), calls=%async_computation.5 | async-start | bytes 2359296 | tf_op jit(solution)/shard_map/all_gather | solution.py:94
  101.5 171.8 %all-gather.13.cloned.1.call-start = ((), (), s32[]{:S(2)}) async-start(), calls=%async_computation.6 | async-start | bytes 4456448 | tf_op jit(solution)/shard_map/all_gather | solution.py:93
  102.1 199.2 %all-gather.15.cloned.1.call-start = ((), (), s32[]{:S(2)}) async-start(), calls=%async_computation.7 | async-start | bytes 2359296 | tf_op jit(solution)/shard_map/all_gather | solution.py:94
  103.2 257.5 %all-gather.17.cloned.1.call-start = ((), (), s32[]{:S(2)}) async-start(), calls=%async_computation.8 | async-start | bytes 4456448 | tf_op jit(solution)/shard_map/all_gather | solution.py:93
  185.2 95.3 %copy-start = (bf16[129,64,128]{2,1,0:T(8,128)(2,1)S(1)}, bf16[129,64,128]{2,1,0:T(8,128)(2,1)}, u32[]{:S(2)}) copy-start(bf16[129,64,128]{2,1,0:T(8,128)(2,1)} %all-gather.7.cloned.1.call-done) | copy-start | bytes 6340612
  273.3 7.3 %copy-start.1 = (bf16[128,128,128]{2,1,0:T(8,128)(2,1)S(1)}, bf16[128,128,128]{2,1,0:T(8,128)(2,1)}, u32[]{:S(2)}) copy-start(bf16[128,128,128]{2,1,0:T(8,128)(2,1)} %fusion.152) | copy-start | bytes 12582916
  360.7 6.0 %copy-start.2 = (bf16[128,64,128]{0,1,2:T(8,128)(2,1)S(1)}, bf16[128,64,128]{0,1,2:T(8,128)(2,1)}, u32[]{:S(2)}) copy-start(bf16[128,64,128]{0,1,2:T(8,128)(2,1)} %fusion.5) | copy-start | bytes 6291460
  360.7 6.0 %copy-start.3 = (bf16[128,64,128]{0,1,2:T(8,128)(2,1)S(1)}, bf16[128,64,128]{0,1,2:T(8,128)(2,1)}, u32[]{:S(2)}) copy-start(bf16[128,64,128]{0,1,2:T(8,128)(2,1)} %fusion.4) | copy-start | bytes 6291460
Sparse Core Ops, SparseCore 0:
  99.8 55.7 all-gather.8
  157.8 26.4 all-gather.6
  186.0 27.7 all-gather.10
  215.8 57.4 all-gather.12
  274.8 26.3 all-gather.14
  303.2 57.4 all-gather.16

commit v4 on v2

--- a/solution.py
+++ b/solution.py
@@ -74,7 +74,10 @@
     mask_row = jnp.concatenate([mask_float, jnp.zeros_like(mask_float)], axis=1)
     stacked = jnp.concatenate([stacked, mask_row[None]], axis=0)
     left_all = lax.all_gather(stacked, "col", axis=1, tiled=True)
-    right_all = lax.all_gather(stacked, "row", axis=1, tiled=True)
+    rows = lax.axis_size("row")
+    copies = jnp.broadcast_to(stacked[None], (rows,) + stacked.shape)
+    got = lax.all_to_all(copies, "row", split_axis=0, concat_axis=0, tiled=True)
+    right_all = got.transpose(1, 0, 2, 3).reshape(F + 1, rows * owned, 2 * W)
     left, left_mask = left_all[:F], left_all[F, :, :W]
     right, right_mask = right_all[:F], right_all[F, :, :W]
     counts = jnp.dot(left_mask, right_mask.T, preferred_element_type=jnp.float32)

time: 306 us -> 253 us (0.83)
  waiting for transfers between devices: 182 us -> 130 us
  matrix products: 42.7 us -> 36.6 us
  starting transfers between devices: 7.56 us -> 12.6 us
    all_gather x1, waiting for transfers between devices: 101 us -> 13.3 us  [per_device(): left_all = lax.all_gather(stacked, 'col', axis=1, tiled=True)]
    all_to_all x0 -> x1, waiting for transfers between devices: none -> 72.4 us  [per_device(): got = lax.all_to_all(copies, 'row', split_axis=0, concat_axis=0, tiled=True)]
    all_gather x1 -> x0, waiting for transfers between devices: 35.7 us -> none  [per_device(): right_all = lax.all_gather(stacked, 'row', axis=1, tiled=True)]
    dot_general x1 -> x0, local copies, waits for them, and re-layouts: 10.7 us -> none  [per_device(): jnp.einsum('fiw,fjw->ijf', left, right, preferred_element_type=jnp.float32)]
    all_to_all x0 -> x1, local copies, waits for them, and re-layouts: none -> 7.27 us  [per_device(): got = lax.all_to_all(copies, 'row', split_axis=0, concat_axis=0, tiled=True)]
    dot_general x1, matrix products: 20.4 us -> 14.3 us  [per_device(): jnp.einsum('fiw,fjw->ijf', left, right, preferred_element_type=jnp.float32)]
    all_to_all x0 -> x1, starting transfers between devices: none -> 5.31 us  [per_device(): got = lax.all_to_all(copies, 'row', split_axis=0, concat_axis=0, tiled=True)]
    broadcast_in_dim x0 -> x1, local copies, waits for them, and re-layouts: none -> 4.54 us  [per_device(): copies = jnp.broadcast_to(stacked[None], (rows,) + stacked.shape)]
  transfers between devices with their start and end apart: 3 -> 3, of which waited for: 3 -> 3; matrix products, arithmetic and copies ran while one was open for 4% -> 5% of each run, Pallas kernels for 0% -> 0%
where the time goes in v4:
time: 253 us; the launch traced here: 252 us
  waiting for transfers between devices  130 us (51%)
  local copies, waits for them, and re-layouts  42.3 us (17%)
  matrix products  36.6 us (14%)
  other arithmetic  14.9 us (6%)
  between operations  14.9 us (6%)
  starting transfers between devices  12.6 us (5%)
    all_to_all x1, waiting for transfers between devices, per_device(): got = lax.all_to_all(copies, 'row', split_axis=0, concat_axis=0, tiled=True)  72.4 us
    all_to_all x1, waiting for transfers between devices, per_device(): lax.all_to_all(payload, 'col', split_axis=0, concat_axis=0, tiled=True)  44.6 us
    unnamed x4, local copies, waits for them, and re-layouts  19.4 us
    dot_general x1, matrix products, per_device(): jnp.einsum('fiw,fjw->ijf', left, right, preferred_element_type=jnp.float32)  14.3 us
    dot_general x1, matrix products, per_device(): jnp.einsum('fiw,fjw->ijf', left, turned, preferred_element_type=jnp.float32)  14.1 us
    all_gather x1, waiting for transfers between devices, per_device(): left_all = lax.all_gather(stacked, 'col', axis=1, tiled=True)  13.3 us
    all_to_all x1, starting transfers between devices, per_device(): lax.all_to_all(payload, 'col', split_axis=0, concat_axis=0, tiled=True)  7.3 us
    dot_general x1, matrix products, whiten(): jnp.dot(segments.reshape(count * W, L), table, preferred_element_type=jnp...  7.29 us
  transfers between devices with their start and end apart: 3, of which 3 were waited for; matrix products, arithmetic and copies ran while one was open for 5% of the time, Pallas kernels for 0%

profile of v4, /device:TPU:0, one launch (start us, length us, event | category | flops | bytes accessed | tf_op | source)
XLA Modules:
  0.0 251.6 jit_solution(1237658847715348398)
XLA Ops:
  7.8 0.7 fusion.51
  8.5 0.1 fusion.50
  8.6 0.2 select_reduce_fusion.2
  8.8 0.1 select_reduce_fusion.1
  8.9 0.1 reduce_sum.53
  9.0 0.1 broadcast_in_dim.119
  9.1 0.1 broadcast_in_dim.120
  9.2 0.1 convert_element_type.82
  9.3 0.4 fusion.31
  9.7 0.4 fusion.38
  10.1 2.0 subtract_convert_fusion
  12.1 7.3 %fusion.20 = f32[1024,768]{0,1:T(8,128)S(1)} fusion(bf16[1024,3072]{1,0:T(8,128)(2,1)} %bitcast.83, bf16[3072,384]{1,0:T(8,128)(2,1)S(1)} %bitcast.82, bf16[3072,384]{1,0:T(8,128)(2,1)S(1)} %bitcast.81), kind=kOutput, calls=%fused_computation.27 | convolution fusion | flops 4841275392 | bytes 14155776 | tf_op jit(solution)/shard_map/dot_general | solution.py:32
  19.4 1.5 multiply_add_fusion
  20.9 1.6 reduce_sum.54
  22.5 1.6 fusion.23
  24.0 1.5 copy.39
  25.5 1.5 copy.40
  27.0 0.2 pad_maximum_fusion
  27.2 2.4 gather_fusion
  29.6 2.1 bitcast_select_fusion
  31.7 2.0 fusion.13
  33.7 0.0 copy-start
  33.7 7.3 %all-to-all-start = ((bf16[16,136,768]{2,1,0:T(8,128)(2,1)}), bf16[16,136,768]{2,1,0:T(8,128)(2,1)S(1)}, u32[]{:S(2)}, u32[]{:S(2)}) async-start(bf16[16,136,768]{2,1,0:T(8,128)(2,1)} %fusion.13), calls=%async_computation | async-start | bytes 6684672 | tf_op jit(solution)/shard_map/all_to_all | solution.py:65
  41.0 0.0 all-gather.2.cloned.1.call-start
  41.0 0.0 copy-done
  41.1 44.6 %all-to-all-done = bf16[16,136,768]{2,1,0:T(8,128)(2,1)S(1)} async-done(((bf16[16,136,768]{2,1,0:T(8,128)(2,1)}), bf16[16,136,768]{2,1,0:T(8,128)(2,1)S(1)}, u32[]{:S(2)}, u32[]{:S(2)}) %all-to-all-start) | async-done | bytes 3342368 | tf_op jit(solution)/shard_map/all_to_all | solution.py:65
  85.7 0.1 reshape.313
  85.8 0.1 select_reduce_fusion.3
  86.0 2.0 slice.66
  87.9 2.5 gather_fusion.1
  90.4 0.2 gather.15
  90.6 1.0 multiply_bitcast_fusion
  91.7 0.1 copy.42
  91.8 0.5 copy.43
  92.3 0.9 pad_maximum_fusion.1
  93.3 0.0 all-gather.2.cloned.1.call-update
  93.3 4.5 %broadcast_in_dim.130 = bf16[8,385,8,128]{3,2,1,0:T(8,128)(2,1)} broadcast(bf16[385,8,128]{2,1,0:T(8,128)(2,1)} %pad_maximum_fusion.1), dimensions={1,2,3} | broadcast | bytes 7096320 | tf_op jit(solution)/shard_map/broadcast_in_dim | solution.py:78
  97.8 5.3 %all-to-all-start.1 = ((bf16[8,385,8,128]{3,2,1,0:T(8,128)(2,1)}), bf16[8,385,8,128]{3,2,1,0:T(8,128)(2,1)}, u32[]{:S(2)}, u32[]{:S(2)}) async-start(bf16[8,385,8,128]{3,2,1,0:T(8,128)(2,1)} %broadcast_in_dim.130), calls=%async_computation.1 | async-start | bytes 12615680 | tf_op jit(solution)/shard_map/all_to_all | solution.py:79
  103.2 72.4 %all-to-all-done.1 = bf16[8,385,8,128]{3,2,1,0:T(8,128)(2,1)} async-done(((bf16[8,385,8,128]{3,2,1,0:T(8,128)(2,1)}), bf16[8,385,8,128]{3,2,1,0:T(8,128)(2,1)}, u32[]{:S(2)}, u32[]{:S(2)}) %all-to-all-start.1) | async-done | bytes 6307872 | tf_op jit(solution)/shard_map/all_to_all | solution.py:79
  175.5 7.3 %copy.49 = bf16[8,385,8,128]{3,2,0,1:T(8,128)(2,1)} copy(bf16[8,385,8,128]{3,2,1,0:T(8,128)(2,1)} %all-to-all-done.1) | data formatting | bytes 12615680 | tf_op jit(solution)/shard_map/all_to_all | solution.py:79
  182.8 13.3 %all-gather.2.cloned.1.call-done = bf16[385,128,128]{2,1,0:T(8,128)(2,1)} async-done(((bf16[385,8,128]{2,1,0:T(8,128)(2,1)}), bf16[385,128,128]{2,1,0:T(8,128)(2,1)}) %all-gather.2.cloned.1.call-update) | async-done | bytes 12615696 | tf_op jit(solution)/shard_map/all_gather | solution.py:76
  196.1 0.9 fusion.25
  197.0 14.3 %fusion.1 = bf16[128,64,384]{0,1,2:T(8,128)(2,1)} fusion(f32[128,64]{0,1:T(8,128)S(1)} %fusion.25, bf16[385,128,128]{2,1,0:T(8,128)(2,1)} %all-gather.2.cloned.1.call-done, bf16[385,8,8,128]{3,2,1,0:T(8,128)(2,1)} %bitcast.74), kind=kOutput, calls=%fused_computation.5 | convolution fusion | flops 811597824 | bytes 25198592 | tf_op jit(solution)/shard_map/fiw,fjw->ijf/dot_general | solution.py:94
  211.4 9.7 %copy.45 = bf16[128,64,384]{2,1,0:T(8,128)(2,1)} copy(bf16[128,64,384]{0,1,2:T(8,128)(2,1)} %fusion.1) | data formatting | bytes 12582912
  221.0 14.1 %fusion = bf16[128,64,384]{0,1,2:T(8,128)(2,1)} fusion(f32[128,64]{0,1:T(8,128)S(1)} %fusion.25, bf16[385,128,128]{2,1,0:T(8,128)(2,1)} %all-gather.2.cloned.1.call-done, bf16[385,8,8,128]{3,2,1,0:T(8,128)(2,1)} %bitcast.75, bf16[128]{0:T(256)(128)(2,1)S(1)} %compare_select_fusion.8, s32[128]{0:T(128)S(1)} %and_select_fusion), kind=kOutput, calls=%fused_computation.3 | convolution fusion | flops 1620082688 | bytes 25199360 | tf_op jit(solution)/shard_map/fiw,fjw->ijf/dot_general | solution.py:95
  235.1 9.7 %copy.46 = bf16[128,64,384]{2,1,0:T(8,128)(2,1)} copy(bf16[128,64,384]{0,1,2:T(8,128)(2,1)} %fusion) | data formatting | bytes 12582912
  (17 shorter events, 0.2 us)
Async XLA Ops:
  33.7 7.4 %copy-start = (s32[8,64]{1,0:T(8,128)S(1)}, s32[8,64]{1,0:T(8,128)}, u32[]{:S(2)}) copy-start(s32[8,64]{1,0:T(8,128)} %param.9) | copy-start | bytes 6148
  33.7 52.0 %all-to-all-start = ((bf16[16,136,768]{2,1,0:T(8,128)(2,1)}), bf16[16,136,768]{2,1,0:T(8,128)(2,1)S(1)}, u32[]{:S(2)}, u32[]{:S(2)}) async-start(bf16[16,136,768]{2,1,0:T(8,128)(2,1)} %fusion.13), calls=%async_computation | async-start | bytes 6684672 | tf_op jit(solution)/shard_map/all_to_all | solution.py:65
  41.0 155.1 %all-gather.2.cloned.1.call-start = ((), (), s32[]{:S(2)}) async-start(), calls=%async_computation.2 | async-start | bytes 13404160 | tf_op jit(solution)/shard_map/all_gather | solution.py:76
  97.8 77.7 %all-to-all-start.1 = ((bf16[8,385,8,128]{3,2,1,0:T(8,128)(2,1)}), bf16[8,385,8,128]{3,2,1,0:T(8,128)(2,1)}, u32[]{:S(2)}, u32[]{:S(2)}) async-start(bf16[8,385,8,128]{3,2,1,0:T(8,128)(2,1)} %broadcast_in_dim.130), calls=%async_computation.1 | async-start | bytes 12615680 | tf_op jit(solution)/shard_map/all_to_all | solution.py:79
Sparse Core Ops, SparseCore 0:
  93.4 102.6 all-gather.1

commit v5 on v4

--- a/solution.py
+++ b/solution.py
@@ -91,11 +91,11 @@
     turned = jnp.einsum("fjw,wv->fjv", right, swap, preferred_element_type=jnp.float32).astype(
         jnp.bfloat16
     )
-    real = jnp.einsum("fiw,fjw->ijf", left, right, preferred_element_type=jnp.float32)
-    imag = jnp.einsum("fiw,fjw->ijf", left, turned, preferred_element_type=jnp.float32)
-    real_part = (real * inverse[:, :, None]).astype(jnp.bfloat16)
-    imag_part = (imag * inverse[:, :, None]).astype(jnp.bfloat16)
-    return (real_part, imag_part)
+    across = right.shape[1]
+    both = jnp.concatenate([right, turned], axis=1)
+    product = jnp.einsum("fiw,fjw->ijf", left, both, preferred_element_type=jnp.float32)
+    scaled = (product * jnp.concatenate([inverse, inverse], axis=1)[:, :, None]).astype(jnp.bfloat16)
+    return (scaled[:, :across], scaled[:, across:])
 
 
 def solution(mesh):

time: 253 us -> 254 us (level)
  local copies, waits for them, and re-layouts: 42.3 us -> 55.9 us
  matrix products: 36.6 us -> 29.9 us
  waiting for transfers between devices: 130 us -> 124 us
    slice x0 -> x2, local copies, waits for them, and re-layouts: none -> 16.2 us  [the longest x1 11.5 us: per_device(): return (scaled[:, :across], scaled[:, across:])]
    dot_general x2, matrix products: 28.4 us -> 21.7 us  [the longest x1 18 us: per_device(): jnp.einsum('fiw,fjw->ijf', left, both, preferred_element_type=jnp.float32)]
    all_gather x1, waiting for transfers between devices: 13.3 us -> 7.45 us  [per_device(): left_all = lax.all_gather(stacked, 'col', axis=1, tiled=True)]
    all_to_all x1, local copies, waits for them, and re-layouts: 7.27 us -> 4.67 us  [per_device(): got = lax.all_to_all(copies, 'row', split_axis=0, concat_axis=0, tiled=True)]
    unnamed x4 -> x6, local copies, waits for them, and re-layouts: 19.4 us -> 19.4 us
  transfers between devices with their start and end apart: 3 -> 3, of which waited for: 3 -> 3; matrix products, arithmetic and copies ran while one was open for 5% -> 7% of each run, Pallas kernels for 0% -> 0%
where the time goes in v5:
time: 254 us; the launch traced here: 253 us
  waiting for transfers between devices  124 us (49%)
  local copies, waits for them, and re-layouts  55.9 us (22%)
  matrix products  29.9 us (12%)
  other arithmetic  15 us (6%)
  between operations  14.9 us (6%)
  starting transfers between devices  12.6 us (5%)
    all_to_all x1, waiting for transfers between devices, per_device(): got = lax.all_to_all(copies, 'row', split_axis=0, concat_axis=0, tiled=True)  72.4 us
    all_to_all x1, waiting for transfers between devices, per_device(): lax.all_to_all(payload, 'col', split_axis=0, concat_axis=0, tiled=True)  44.6 us
    unnamed x6, local copies, waits for them, and re-layouts  19.4 us
    dot_general x1, matrix products, per_device(): jnp.einsum('fiw,fjw->ijf', left, both, preferred_element_type=jnp.float32)  18 us
    slice x1, local copies, waits for them, and re-layouts, per_device(): return (scaled[:, :across], scaled[:, across:])  11.5 us
    all_gather x1, waiting for transfers between devices, per_device(): left_all = lax.all_gather(stacked, 'col', axis=1, tiled=True)  7.45 us
    all_to_all x1, starting transfers between devices, per_device(): lax.all_to_all(payload, 'col', split_axis=0, concat_axis=0, tiled=True)  7.3 us
    dot_general x1, matrix products, whiten(): jnp.dot(segments.reshape(count * W, L), table, preferred_element_type=jnp...  7.29 us
  transfers between devices with their start and end apart: 3, of which 3 were waited for; matrix products, arithmetic and copies ran while one was open for 7% of the time, Pallas kernels for 0%

profile of v5, /device:TPU:0, one launch (start us, length us, event | category | flops | bytes accessed | tf_op | source)
XLA Modules:
  0.0 252.8 jit_solution(16616829915455835744)
XLA Ops:
  7.8 0.7 fusion.43
  8.5 0.1 fusion.42
  8.6 0.2 select_reduce_fusion.2
  8.8 0.1 select_reduce_fusion.1
  8.9 0.1 reduce_sum.53
  9.0 0.1 broadcast_in_dim.118
  9.1 0.1 broadcast_in_dim.119
  9.2 0.1 convert_element_type.78
  9.3 0.4 fusion.27
  9.7 0.4 fusion.34
  10.1 2.0 subtract_convert_fusion
  12.1 7.3 %fusion.16 = f32[1024,768]{0,1:T(8,128)S(1)} fusion(bf16[1024,3072]{1,0:T(8,128)(2,1)} %bitcast.69, bf16[3072,384]{1,0:T(8,128)(2,1)S(1)} %bitcast.68, bf16[3072,384]{1,0:T(8,128)(2,1)S(1)} %bitcast.67), kind=kOutput, calls=%fused_computation.25 | convolution fusion | flops 4841275392 | bytes 14155776 | tf_op jit(solution)/shard_map/dot_general | solution.py:32
  19.4 1.5 multiply_add_fusion
  20.9 1.6 reduce_sum.54
  22.5 1.6 fusion.19
  24.0 1.5 copy.39
  25.5 1.5 copy.40
  27.0 0.2 pad_maximum_fusion
  27.2 2.4 gather_fusion
  29.6 2.1 bitcast_select_fusion
  31.7 2.0 fusion.15
  33.7 7.3 %all-to-all-start = ((bf16[16,136,768]{2,1,0:T(8,128)(2,1)}), bf16[16,136,768]{2,1,0:T(8,128)(2,1)S(1)}, u32[]{:S(2)}, u32[]{:S(2)}) async-start(bf16[16,136,768]{2,1,0:T(8,128)(2,1)} %fusion.15), calls=%async_computation | async-start | bytes 6684672 | tf_op jit(solution)/shard_map/all_to_all | solution.py:65
  41.0 0.0 all-gather.2.cloned.1.call-start
  41.0 0.0 copy-done.1
  41.1 44.6 %all-to-all-done = bf16[16,136,768]{2,1,0:T(8,128)(2,1)S(1)} async-done(((bf16[16,136,768]{2,1,0:T(8,128)(2,1)}), bf16[16,136,768]{2,1,0:T(8,128)(2,1)S(1)}, u32[]{:S(2)}, u32[]{:S(2)}) %all-to-all-start) | async-done | bytes 3342368 | tf_op jit(solution)/shard_map/all_to_all | solution.py:65
  85.7 0.1 reshape.313
  85.8 0.1 select_reduce_fusion.3
  86.0 2.0 slice.74
  87.9 2.5 gather_fusion.1
  90.4 0.2 gather.15
  90.6 1.0 multiply_bitcast_fusion
  91.7 0.1 copy.42
  91.8 0.5 copy.43
  92.3 1.0 pad_maximum_fusion.1
  93.3 0.0 all-gather.2.cloned.1.call-update
  93.4 4.5 %broadcast_in_dim.129 = bf16[8,385,8,128]{3,2,1,0:T(8,128)(2,1)} broadcast(bf16[385,8,128]{2,1,0:T(8,128)(2,1)} %pad_maximum_fusion.1), dimensions={1,2,3} | broadcast | bytes 7096320 | tf_op jit(solution)/shard_map/broadcast_in_dim | solution.py:78
  97.9 5.3 %all-to-all-start.1 = ((bf16[8,385,8,128]{3,2,1,0:T(8,128)(2,1)}), bf16[8,385,8,128]{3,2,1,0:T(8,128)(2,1)}, u32[]{:S(2)}, u32[]{:S(2)}) async-start(bf16[8,385,8,128]{3,2,1,0:T(8,128)(2,1)} %broadcast_in_dim.129), calls=%async_computation.1 | async-start | bytes 12615680 | tf_op jit(solution)/shard_map/all_to_all | solution.py:79
  103.2 72.4 %all-to-all-done.1 = bf16[8,385,8,128]{3,2,1,0:T(8,128)(2,1)} async-done(((bf16[8,385,8,128]{3,2,1,0:T(8,128)(2,1)}), bf16[8,385,8,128]{3,2,1,0:T(8,128)(2,1)}, u32[]{:S(2)}, u32[]{:S(2)}) %all-to-all-start.1) | async-done | bytes 6307872 | tf_op jit(solution)/shard_map/all_to_all | solution.py:79
  175.6 4.7 %copy.49 = bf16[8,385,8,128]{3,2,0,1:T(8,128)(2,1)S(1)} copy(bf16[8,385,8,128]{3,2,1,0:T(8,128)(2,1)} %all-to-all-done.1) | data formatting | bytes 12615680 | tf_op jit(solution)/shard_map/all_to_all | solution.py:79
  180.3 0.0 copy-start
  180.3 4.8 %slice_bitcast_fusion = bf16[384,64,128]{2,1,0:T(8,128)(2,1)} fusion(bf16[385,8,8,128]{3,2,1,0:T(8,128)(2,1)S(1)} %bitcast.58), kind=kLoop, calls=%fused_computation.11 | loop fusion | bytes 12582912 | tf_op jit(solution)/shard_map/slice | solution.py:82
  185.1 3.7 %convolution_convert_fusion = bf16[384,64,128]{2,1,0:T(8,128)(2,1)} fusion(bf16[128]{0:T(256)(128)(2,1)S(1)} %compare_select_fusion.8, s32[128]{0:T(128)S(1)} %and_select_fusion, bf16[385,8,8,128]{3,2,1,0:T(8,128)(2,1)S(1)} %bitcast.59), kind=kOutput, calls=%fused_computation.20 | convolution fusion | flops 808484864 | bytes 12583936 | tf_op jit(solution)/shard_map/fjw,wv->fjv/dot_general | solution.py:91
  188.7 7.5 %all-gather.2.cloned.1.call-done = bf16[385,128,128]{2,1,0:T(8,128)(2,1)} async-done(((bf16[385,8,128]{2,1,0:T(8,128)(2,1)}), bf16[385,128,128]{2,1,0:T(8,128)(2,1)}) %all-gather.2.cloned.1.call-update) | async-done | bytes 12615696 | tf_op jit(solution)/shard_map/all_gather | solution.py:76
  196.2 0.9 fusion.21
  197.1 18.0 %fusion = bf16[128,128,384]{0,1,2:T(8,128)(2,1)} fusion(f32[128,128]{0,1:T(8,128)S(1)} %pad_maximum_fusion.2, bf16[385,128,128]{2,1,0:T(8,128)(2,1)} %all-gather.2.cloned.1.call-done, bf16[384,64,128]{2,1,0:T(8,128)(2,1)} %convolution_convert_fusion, bf16[384,64,128]{2,1,0:T(8,128)(2,1)} %slice_bitcast_fusion), kind=kOutput, calls=%fused_computation.3 | convolution fusion | flops 1648361472 | bytes 37814272 | tf_op jit(solution)/shard_map/fiw,fjw->ijf/dot_general | solution.py:96
  215.1 11.5 %fusion.51 = (bf16[128,64,384]{0,1,2:T(8,128)(2,1)}, bf16[128,64,384]{0,1,2:T(8,128)(2,1)}) fusion(bf16[128,128,384]{0,1,2:T(8,128)(2,1)} %fusion), kind=kLoop, calls=%fused_computation.107 | loop fusion | bytes 25165824 | tf_op jit(solution)/shard_map/slice | solution.py:98
  226.6 9.7 %copy.46 = bf16[128,64,384]{2,1,0:T(8,128)(2,1)} copy(bf16[128,64,384]{0,1,2:T(8,128)(2,1)} %get-tuple-element.28) | data formatting | bytes 12582912
  236.3 9.7 %copy.45 = bf16[128,64,384]{2,1,0:T(8,128)(2,1)} copy(bf16[128,64,384]{0,1,2:T(8,128)(2,1)} %get-tuple-element.29) | data formatting | bytes 12582912
  (20 shorter events, 0.2 us)
Async XLA Ops:
  33.7 7.4 %copy-start.1 = (s32[8,64]{1,0:T(8,128)S(1)}, s32[8,64]{1,0:T(8,128)}, u32[]{:S(2)}) copy-start(s32[8,64]{1,0:T(8,128)} %param.9) | copy-start | bytes 6148
  33.7 52.0 %all-to-all-start = ((bf16[16,136,768]{2,1,0:T(8,128)(2,1)}), bf16[16,136,768]{2,1,0:T(8,128)(2,1)S(1)}, u32[]{:S(2)}, u32[]{:S(2)}) async-start(bf16[16,136,768]{2,1,0:T(8,128)(2,1)} %fusion.15), calls=%async_computation | async-start | bytes 6684672 | tf_op jit(solution)/shard_map/all_to_all | solution.py:65
  41.0 155.2 %all-gather.2.cloned.1.call-start = ((), (), s32[]{:S(2)}) async-start(), calls=%async_computation.2 | async-start | bytes 13404160 | tf_op jit(solution)/shard_map/all_gather | solution.py:76
  97.9 77.7 %all-to-all-start.1 = ((bf16[8,385,8,128]{3,2,1,0:T(8,128)(2,1)}), bf16[8,385,8,128]{3,2,1,0:T(8,128)(2,1)}, u32[]{:S(2)}, u32[]{:S(2)}) async-start(bf16[8,385,8,128]{3,2,1,0:T(8,128)(2,1)} %broadcast_in_dim.129), calls=%async_computation.1 | async-start | bytes 12615680 | tf_op jit(solution)/shard_map/all_to_all | solution.py:79
  180.3 4.8 %copy-start = (bf16[8,385,8,128]{3,2,0,1:T(8,128)(2,1)}, bf16[8,385,8,128]{3,2,0,1:T(8,128)(2,1)S(1)}, u32[]{:S(2)}) copy-start(bf16[8,385,8,128]{3,2,0,1:T(8,128)(2,1)S(1)} %copy.49) | copy-start | bytes 18923524
Sparse Core Ops, SparseCore 0:
  93.5 102.6 all-gather.1

commit v6 on v5

--- a/solution.py
+++ b/solution.py
@@ -3,6 +3,8 @@
 import jax
 import jax.numpy as jnp
 from jax import lax
+from jax.experimental import pallas as pl
+from jax.experimental.pallas import tpu as pltpu
 from jax.sharding import PartitionSpec as P
 
 F = 384
@@ -11,6 +13,56 @@
 BAND = 64
 CAP = 2
 W = 64
+
+
+FB = 128
+
+def cross_kernel(l_ref, r_ref, inv_ref, re_ref, im_ref, acc_ref):
+    ni = l_ref.shape[1]
+    nj = r_ref.shape[1]
+    half = r_ref.shape[2] // 2
+    lane = lax.broadcasted_iota(jnp.int32, (nj, 2 * half), 1)
+    sign = jnp.where(lane < half, 1.0, -1.0).astype(jnp.float32)
+
+    def per_f(f, carry):
+        rf = r_ref[f]
+        tf = (pltpu.roll(rf.astype(jnp.float32), half, 1) * sign).astype(rf.dtype)
+        both = jnp.concatenate([rf, tf], axis=0)
+        res = lax.dot_general(l_ref[f], both, (((1,), (1,)), ((), ())),
+                              preferred_element_type=jnp.float32)
+        acc_ref[pl.ds(pl.multiple_of(f * ni, ni), ni), :] = res
+        return carry
+
+    lax.fori_loop(0, FB, per_f, 0)
+
+    def per_i(i, carry):
+        x = acc_ref[pl.ds(i, FB, stride=ni), :]
+        y = (x * inv_ref[pl.ds(i, 1), :]).T
+        re_ref[i] = y[:nj].astype(re_ref.dtype)
+        im_ref[i] = y[nj:].astype(im_ref.dtype)
+        return carry
+
+    lax.fori_loop(0, ni, per_i, 0)
+
+
+def cross(left, right, inverse2, nf):
+    ni, nj, w2 = left.shape[1], right.shape[1], left.shape[2]
+    out = jax.ShapeDtypeStruct((ni, nj, nf), jnp.bfloat16)
+    return pl.pallas_call(
+        cross_kernel,
+        grid=(nf // FB,),
+        in_specs=[
+            pl.BlockSpec((FB, ni, w2), lambda f: (f, 0, 0)),
+            pl.BlockSpec((FB, nj, w2), lambda f: (f, 0, 0)),
+            pl.BlockSpec((ni, 2 * nj), lambda f: (0, 0)),
+        ],
+        out_specs=[
+            pl.BlockSpec((ni, nj, FB), lambda f: (0, 0, f)),
+            pl.BlockSpec((ni, nj, FB), lambda f: (0, 0, f)),
+        ],
+        out_shape=[out, out],
+        scratch_shapes=[pltpu.VMEM((FB * ni, 2 * nj), jnp.float32)],
+    )(left, right, inverse2)
 
 
 def transform_table():
@@ -78,24 +130,11 @@
     copies = jnp.broadcast_to(stacked[None], (rows,) + stacked.shape)
     got = lax.all_to_all(copies, "row", split_axis=0, concat_axis=0, tiled=True)
     right_all = got.transpose(1, 0, 2, 3).reshape(F + 1, rows * owned, 2 * W)
-    left, left_mask = left_all[:F], left_all[F, :, :W]
-    right, right_mask = right_all[:F], right_all[F, :, :W]
+    left_mask = left_all[F, :, :W]
+    right_mask = right_all[F, :, :W]
     counts = jnp.dot(left_mask, right_mask.T, preferred_element_type=jnp.float32)
     inverse = 1.0 / jnp.maximum(counts, 1.0)
-    lane = jnp.arange(2 * W, dtype=jnp.int32)
-    swap = jnp.where(
-        lane[:, None] == (lane[None, :] + W) % (2 * W),
-        jnp.where(lane[None, :] < W, 1.0, -1.0),
-        0.0,
-    ).astype(jnp.bfloat16)
-    turned = jnp.einsum("fjw,wv->fjv", right, swap, preferred_element_type=jnp.float32).astype(
-        jnp.bfloat16
-    )
-    across = right.shape[1]
-    both = jnp.concatenate([right, turned], axis=1)
-    product = jnp.einsum("fiw,fjw->ijf", left, both, preferred_element_type=jnp.float32)
-    scaled = (product * jnp.concatenate([inverse, inverse], axis=1)[:, :, None]).astype(jnp.bfloat16)
-    return (scaled[:, :across], scaled[:, across:])
+    return tuple(cross(left_all, right_all, jnp.concatenate([inverse, inverse], axis=1), F))
 
 
 def solution(mesh):

time: 254 us -> 344 us (1.35)
  Pallas kernels: 0 us -> 139 us
  blocking collectives: 0 us -> 77.4 us
  waiting for transfers between devices: 124 us -> 63.6 us
  local copies, waits for them, and re-layouts: 55.9 us -> 17.5 us
  matrix products: 29.9 us -> 8.2 us
  starting transfers between devices: 12.6 us -> 7.32 us
    pallas_call x0 -> x1, Pallas kernels: none -> 139 us  [cross(): pl.pallas_call(cross_kernel, grid=(nf // FB,), in_specs=[pl.BlockSpec((FB...]
    all_to_all x0 -> x1, blocking collectives: none -> 77.4 us  [per_device(): got = lax.all_to_all(copies, 'row', split_axis=0, concat_axis=0, tiled=True)]
    all_to_all x1 -> x0, waiting for transfers between devices: 72.4 us -> none  [per_device(): got = lax.all_to_all(copies, 'row', split_axis=0, concat_axis=0, tiled=True)]
    dot_general x2 -> x0, matrix products: 21.7 us -> none  [the longest x1 18 us: per_device(): jnp.einsum('fiw,fjw->ijf', left, both, preferred_element_type=jnp.float32)]
    unnamed x6 -> x2, local copies, waits for them, and re-layouts: 19.4 us -> 0.01 us
    slice x2 -> x0, local copies, waits for them, and re-layouts: 16.2 us -> none  [the longest x1 11.5 us: per_device(): return (scaled[:, :across], scaled[:, across:])]
    all_gather x1, waiting for transfers between devices: 7.45 us -> 19 us  [per_device(): left_all = lax.all_gather(stacked, 'col', axis=1, tiled=True)]
    all_to_all x1 -> x0, starting transfers between devices: 5.31 us -> none  [per_device(): got = lax.all_to_all(copies, 'row', split_axis=0, concat_axis=0, tiled=True)]
  transfers between devices with their start and end apart: 3 -> 2, of which waited for: 3 -> 2; matrix products, arithmetic and copies ran while one was open for 7% -> 2% of each run, Pallas kernels for 0% -> 0%
where the time goes in v6:
time: 344 us
  Pallas kernels  139 us (40%)
  blocking collectives  77.4 us (23%)
  waiting for transfers between devices  63.6 us (18%)
  local copies, waits for them, and re-layouts  17.5 us (5%)
  other arithmetic  15.6 us (5%)
  between operations  14.9 us (4%)
  matrix products  8.2 us (2%)
  starting transfers between devices  7.32 us (2%)
    pallas_call x1, Pallas kernels, cross(): pl.pallas_call(cross_kernel, grid=(nf // FB,), in_specs=[pl.BlockSpec((FB...  139 us
    all_to_all x1, blocking collectives, per_device(): got = lax.all_to_all(copies, 'row', split_axis=0, concat_axis=0, tiled=True)  77.4 us
    all_to_all x1, waiting for transfers between devices, per_device(): lax.all_to_all(payload, 'col', split_axis=0, concat_axis=0, tiled=True)  44.6 us
    all_gather x1, waiting for transfers between devices, per_device(): left_all = lax.all_gather(stacked, 'col', axis=1, tiled=True)  19 us
    dot_general x1, matrix products, whiten(): jnp.dot(segments.reshape(count * W, L), table, preferred_element_type=jnp...  7.29 us
    all_to_all x1, starting transfers between devices, per_device(): lax.all_to_all(payload, 'col', split_axis=0, concat_axis=0, tiled=True)  7.28 us
  transfers between devices with their start and end apart: 2, of which 2 were waited for; matrix products, arithmetic and copies ran while one was open for 2% of the time, Pallas kernels for 0%

profile of v6, /device:TPU:0, one launch (start us, length us, event | category | flops | bytes accessed | tf_op | source)
XLA Modules:
  0.0 343.7 jit_solution(12962297531308591156)
XLA Ops:
  7.8 0.7 fusion.28
  8.5 0.1 fusion.27
  8.6 0.2 select_reduce_fusion.2
  8.8 0.1 select_reduce_fusion.1
  8.9 0.1 reduce_sum.53
  9.0 0.1 broadcast_in_dim.94
  9.1 0.1 broadcast_in_dim.95
  9.2 0.1 convert_element_type.66
  9.3 0.4 fusion.17
  9.7 0.4 fusion.24
  10.1 2.0 subtract_convert_fusion
  12.1 7.3 %fusion.6 = f32[1024,768]{0,1:T(8,128)S(1)} fusion(bf16[1024,3072]{1,0:T(8,128)(2,1)} %bitcast.55, bf16[3072,384]{1,0:T(8,128)(2,1)S(1)} %bitcast.54, bf16[3072,384]{1,0:T(8,128)(2,1)S(1)} %bitcast.53), kind=kOutput, calls=%fused_computation.15 | convolution fusion | flops 4841275392 | bytes 14155776 | tf_op jit(solution)/shard_map/dot_general | solution.py:84
  19.4 1.5 multiply_add_fusion
  20.9 1.6 reduce_sum.54
  22.5 1.6 fusion.9
  24.0 1.5 copy.34
  25.5 1.5 copy.35
  27.0 0.2 pad_maximum_fusion
  27.2 2.4 gather_fusion
  29.6 2.1 bitcast_select_fusion
  31.7 2.0 fusion.5
  33.7 0.0 copy-start
  33.7 7.3 %all-to-all-start = ((bf16[16,136,768]{2,1,0:T(8,128)(2,1)}), bf16[16,136,768]{2,1,0:T(8,128)(2,1)S(1)}, u32[]{:S(2)}, u32[]{:S(2)}) async-start(bf16[16,136,768]{2,1,0:T(8,128)(2,1)} %fusion.5), calls=%async_computation | async-start | bytes 6684672 | tf_op jit(solution)/shard_map/all_to_all | solution.py:117
  41.0 0.0 all-gather.2.cloned.1.call-start
  41.0 0.0 copy-done
  41.1 44.6 %all-to-all-done = bf16[16,136,768]{2,1,0:T(8,128)(2,1)S(1)} async-done(((bf16[16,136,768]{2,1,0:T(8,128)(2,1)}), bf16[16,136,768]{2,1,0:T(8,128)(2,1)S(1)}, u32[]{:S(2)}, u32[]{:S(2)}) %all-to-all-start) | async-done | bytes 3342368 | tf_op jit(solution)/shard_map/all_to_all | solution.py:117
  85.7 0.1 reshape.282
  85.8 0.1 select_reduce_fusion.3
  86.0 2.0 slice.54
  87.9 2.5 gather_fusion.1
  90.4 0.2 gather.15
  90.6 1.0 multiply_bitcast_fusion
  91.7 0.1 copy.37
  91.8 0.5 copy.38
  92.3 0.9 pad_maximum_fusion.1
  93.3 0.0 all-gather.2.cloned.1.call-update
  93.3 1.9 broadcast_in_dim.105
  95.2 77.4 %all_to_all.10 = bf16[8,385,8,128]{3,2,1,0:T(8,128)(2,1)S(1)} all-to-all(bf16[8,385,8,128]{3,2,1,0:T(8,128)(2,1)S(1)} %broadcast_in_dim.105), channel_id=1, replica_groups=mesh['row'=8,'col'=16] {'row'}, dimensions={0} | all-to-all | bytes 12615680 | tf_op jit(solution)/shard_map/all_to_all | solution.py:131
  172.7 4.4 %copy_bitcast_fusion.r_ref = bf16[385,64,128]{2,1,0:T(8,128)(2,1)} fusion(bf16[8,385,8,128]{3,2,1,0:T(8,128)(2,1)S(1)} %all_to_all.10), kind=kLoop, calls=%fused_computation.4 | loop fusion | bytes 12615680 | tf_op jit(solution)/shard_map/reshape | solution.py:132
  177.1 19.0 %all-gather.2.cloned.1.call-done.l_ref = bf16[385,128,128]{2,1,0:T(8,128)(2,1)} async-done(((bf16[385,8,128]{2,1,0:T(8,128)(2,1)}), bf16[385,128,128]{2,1,0:T(8,128)(2,1)}) %all-gather.2.cloned.1.call-update) | async-done | bytes 12615696 | tf_op jit(solution)/shard_map/all_gather | solution.py:128
  196.1 0.9 fusion.11
  197.0 0.7 pad_maximum_fusion.2.inv_ref
  197.7 139.1 %shard_map.59 = (bf16[128,64,384]{2,1,0:T(8,128)(2,1)}, bf16[128,64,384]{2,1,0:T(8,128)(2,1)}) custom-call(bf16[385,128,128]{2,1,0:T(8,128)(2,1)} %all-gather.2.cloned.1.call-done.l_ref, bf16[385,64,128]{2,1,0:T(8,128)(2,1)} %copy_bitcast_fusion.r_ref, f32[128,128]{1,0:T(8,128)} %pad_maximum_fusion.2.inv_ref), custom_call_target="tpu_custom_call" | custom-call | tf_op jit(solution)/shard_map/pallas_call | solution.py:51
  (15 shorter events, 0.2 us)
Async XLA Ops:
  33.7 7.3 %copy-start = (s32[8,64]{1,0:T(8,128)S(1)}, s32[8,64]{1,0:T(8,128)}, u32[]{:S(2)}) copy-start(s32[8,64]{1,0:T(8,128)} %param.9) | copy-start | bytes 6148
  33.7 52.0 %all-to-all-start = ((bf16[16,136,768]{2,1,0:T(8,128)(2,1)}), bf16[16,136,768]{2,1,0:T(8,128)(2,1)S(1)}, u32[]{:S(2)}, u32[]{:S(2)}) async-start(bf16[16,136,768]{2,1,0:T(8,128)(2,1)} %fusion.5), calls=%async_computation | async-start | bytes 6684672 | tf_op jit(solution)/shard_map/all_to_all | solution.py:117
  41.0 155.1 %all-gather.2.cloned.1.call-start = ((), (), s32[]{:S(2)}) async-start(), calls=%async_computation.2 | async-start | bytes 13404160 | tf_op jit(solution)/shard_map/all_gather | solution.py:128
Sparse Core Ops, SparseCore 0:
  93.4 102.5 all-gather.1

commit v7 on v4

--- a/solution.py
+++ b/solution.py
@@ -73,12 +73,16 @@
     stacked = spectra.reshape(owned, W, 2, F).transpose(3, 0, 2, 1).reshape(F, owned, 2 * W)
     mask_row = jnp.concatenate([mask_float, jnp.zeros_like(mask_float)], axis=1)
     stacked = jnp.concatenate([stacked, mask_row[None]], axis=0)
-    left_all = lax.all_gather(stacked, "col", axis=1, tiled=True)
+    share = stacked.reshape((F + 1) * owned, 2 * W)
+    pieces = lax.all_gather(share, "col", axis=0, tiled=True)
+    pieces = pieces.reshape(columns, F + 1, owned, 2 * W)
+    gathered_mask = pieces[:, F, :, :W].reshape(columns * owned, W)
+    left_all = pieces.transpose(1, 0, 2, 3).reshape(F + 1, columns * owned, 2 * W)
     rows = lax.axis_size("row")
     copies = jnp.broadcast_to(stacked[None], (rows,) + stacked.shape)
     got = lax.all_to_all(copies, "row", split_axis=0, concat_axis=0, tiled=True)
     right_all = got.transpose(1, 0, 2, 3).reshape(F + 1, rows * owned, 2 * W)
-    left, left_mask = left_all[:F], left_all[F, :, :W]
+    left, left_mask = left_all[:F], gathered_mask
     right, right_mask = right_all[:F], right_all[F, :, :W]
     counts = jnp.dot(left_mask, right_mask.T, preferred_element_type=jnp.float32)
     inverse = 1.0 / jnp.maximum(counts, 1.0)

time: 253 us -> 245 us (0.968)
  waiting for transfers between devices: 130 us -> 121 us
    all_gather x1, waiting for transfers between devices: 13.3 us -> 4.7 us  [per_device(): pieces = lax.all_gather(share, 'col', axis=0, tiled=True)]
    unnamed x4 -> x6, local copies, waits for them, and re-layouts: 19.4 us -> 19.4 us
where the time goes in v7:
time: 245 us; the launch traced here: 243 us
  waiting for transfers between devices  121 us (49%)
  local copies, waits for them, and re-layouts  44 us (18%)
  matrix products  36.7 us (15%)
  between operations  14.9 us (6%)
  other arithmetic  14.1 us (6%)
  starting transfers between devices  12.6 us (5%)
    all_to_all x1, waiting for transfers between devices, per_device(): got = lax.all_to_all(copies, 'row', split_axis=0, concat_axis=0, tiled=True)  72.4 us
    all_to_all x1, waiting for transfers between devices, per_device(): lax.all_to_all(payload, 'col', split_axis=0, concat_axis=0, tiled=True)  43.7 us
    unnamed x6, local copies, waits for them, and re-layouts  19.4 us
    dot_general x1, matrix products, per_device(): jnp.einsum('fiw,fjw->ijf', left, right, preferred_element_type=jnp.float32)  14.4 us
    dot_general x1, matrix products, per_device(): jnp.einsum('fiw,fjw->ijf', left, turned, preferred_element_type=jnp.float32)  14.1 us
    all_to_all x1, starting transfers between devices, per_device(): lax.all_to_all(payload, 'col', split_axis=0, concat_axis=0, tiled=True)  7.3 us
    dot_general x1, matrix products, whiten(): jnp.dot(segments.reshape(count * W, L), table, preferred_element_type=jnp...  7.29 us
    all_to_all x1, local copies, waits for them, and re-layouts, per_device(): got = lax.all_to_all(copies, 'row', split_axis=0, concat_axis=0, tiled=True)  7.2 us
  transfers between devices with their start and end apart: 3, of which 3 were waited for; matrix products, arithmetic and copies ran while one was open for 5% of the time, Pallas kernels for 0%

profile of v7, /device:TPU:0, one launch (start us, length us, event | category | flops | bytes accessed | tf_op | source)
XLA Modules:
  0.0 243.2 jit_solution(14425550625275058496)
XLA Ops:
  7.8 0.7 fusion.53
  8.5 0.1 fusion.52
  8.6 0.2 select_reduce_fusion.2
  8.8 0.1 select_reduce_fusion.1
  8.9 0.1 reduce_sum.53
  9.0 0.1 broadcast_in_dim.119
  9.1 0.1 broadcast_in_dim.120
  9.2 0.1 convert_element_type.82
  9.3 0.4 fusion.33
  9.7 0.4 fusion.40
  10.1 2.0 subtract_convert_fusion
  12.1 7.3 %fusion.22 = f32[1024,768]{0,1:T(8,128)S(1)} fusion(bf16[1024,3072]{1,0:T(8,128)(2,1)} %bitcast.100, bf16[3072,384]{1,0:T(8,128)(2,1)S(1)} %bitcast.96, bf16[3072,384]{1,0:T(8,128)(2,1)S(1)} %bitcast.95), kind=kOutput, calls=%fused_computation.29 | convolution fusion | flops 4841275392 | bytes 14155776 | tf_op jit(solution)/shard_map/dot_general | solution.py:32
  19.4 1.5 multiply_add_fusion
  20.9 1.6 reduce_sum.54
  22.5 1.6 fusion.25
  24.0 1.5 copy.49
  25.5 1.5 copy.50
  27.0 0.2 pad_maximum_fusion
  27.2 2.4 gather_fusion
  29.6 2.1 bitcast_select_fusion
  31.7 2.0 fusion.15
  33.7 0.0 copy-start.1
  33.7 7.3 %all-to-all-start = ((bf16[16,136,768]{2,1,0:T(8,128)(2,1)}), bf16[16,136,768]{2,1,0:T(8,128)(2,1)S(1)}, u32[]{:S(2)}, u32[]{:S(2)}) async-start(bf16[16,136,768]{2,1,0:T(8,128)(2,1)} %fusion.15), calls=%async_computation | async-start | bytes 6684672 | tf_op jit(solution)/shard_map/all_to_all | solution.py:65
  41.0 0.0 all-gather.2.cloned.1.call-start
  41.0 0.0 copy-done.1
  41.1 0.9 copy.53
  42.0 43.7 %all-to-all-done = bf16[16,136,768]{2,1,0:T(8,128)(2,1)S(1)} async-done(((bf16[16,136,768]{2,1,0:T(8,128)(2,1)}), bf16[16,136,768]{2,1,0:T(8,128)(2,1)S(1)}, u32[]{:S(2)}, u32[]{:S(2)}) %all-to-all-start) | async-done | bytes 3342368 | tf_op jit(solution)/shard_map/all_to_all | solution.py:65
  85.7 0.1 reshape.323
  85.8 0.1 select_reduce_fusion.3
  86.0 2.0 slice.70
  87.9 2.5 %gather_fusion.1 = bf16[8,64,768]{2,1,0:T(8,128)(2,1)S(1)} fusion(bf16[32,64,768]{2,1,0:T(8,128)(2,1)} %bitcast.91, s32[1024]{0:T(1024)S(1)} %pad_clamp_fusion), kind=kCustom, calls=%fused_computation.1 | custom fusion | bytes 1572896 | tf_op jit(solution)/shard_map/jit(_take)/gather | solution.py:70
  90.5 0.2 gather.15
  90.7 1.0 multiply_bitcast_fusion
  91.7 0.1 copy.52
  91.9 0.0 copy-done
  91.9 0.1 pad_maximum_fusion.1
  92.0 1.4 copy.54
  93.4 0.0 all-gather.2.cloned.1.call-update
  93.4 4.5 %broadcast_in_dim.130 = bf16[8,385,8,128]{3,2,1,0:T(8,128)(2,1)} broadcast(bf16[385,8,128]{2,1,0:T(8,128)(2,1)} %copy.54), dimensions={1,2,3} | broadcast | bytes 7096320 | tf_op jit(solution)/shard_map/broadcast_in_dim | solution.py:82
  98.0 5.3 %all-to-all-start.1 = ((bf16[8,385,8,128]{3,2,1,0:T(8,128)(2,1)}), bf16[8,385,8,128]{3,2,1,0:T(8,128)(2,1)}, u32[]{:S(2)}, u32[]{:S(2)}) async-start(bf16[8,385,8,128]{3,2,1,0:T(8,128)(2,1)} %broadcast_in_dim.130), calls=%async_computation.1 | async-start | bytes 12615680 | tf_op jit(solution)/shard_map/all_to_all | solution.py:83
  103.3 72.4 %all-to-all-done.1 = bf16[8,385,8,128]{3,2,1,0:T(8,128)(2,1)} async-done(((bf16[8,385,8,128]{3,2,1,0:T(8,128)(2,1)}), bf16[8,385,8,128]{3,2,1,0:T(8,128)(2,1)}, u32[]{:S(2)}, u32[]{:S(2)}) %all-to-all-start.1) | async-done | bytes 6307872 | tf_op jit(solution)/shard_map/all_to_all | solution.py:83
  175.7 7.2 %copy.74 = bf16[8,385,8,128]{3,2,0,1:T(8,128)(2,1)} copy(bf16[8,385,8,128]{3,2,1,0:T(8,128)(2,1)} %all-to-all-done.1) | data formatting | bytes 12615680 | tf_op jit(solution)/shard_map/all_to_all | solution.py:83
  182.9 4.7 %all-gather.2.cloned.1.call-done = bf16[49280,128]{1,0:T(8,128)(2,1)} async-done(((bf16[3080,128]{1,0:T(8,128)(2,1)}), bf16[49280,128]{1,0:T(8,128)(2,1)}) %all-gather.2.cloned.1.call-update) | async-done | bytes 12615696 | tf_op jit(solution)/shard_map/all_gather | solution.py:77
  187.6 0.9 fusion.27
  188.5 14.4 %fusion.1 = bf16[128,64,384]{0,1,2:T(8,128)(2,1)} fusion(f32[128,64]{0,1:T(8,128)S(1)} %fusion.27, bf16[385,8,8,128]{3,2,1,0:T(8,128)(2,1)} %bitcast.88, bf16[385,16,8,128]{3,2,0,1:T(8,128)(2,1)} %bitcast.98), kind=kOutput, calls=%fused_computation.5 | convolution fusion | flops 811597824 | bytes 25198592 | tf_op jit(solution)/shard_map/fiw,fjw->ijf/dot_general | solution.py:98
  202.9 9.7 %copy.58 = bf16[128,64,384]{2,1,0:T(8,128)(2,1)} copy(bf16[128,64,384]{0,1,2:T(8,128)(2,1)} %fusion.1) | data formatting | bytes 12582912
  212.6 14.1 %fusion = bf16[128,64,384]{0,1,2:T(8,128)(2,1)} fusion(f32[128,64]{0,1:T(8,128)S(1)} %fusion.27, bf16[385,8,8,128]{3,2,1,0:T(8,128)(2,1)} %bitcast.89, bf16[128]{0:T(256)(128)(2,1)S(1)} %compare_select_fusion.8, s32[128]{0:T(128)S(1)} %and_select_fusion, bf16[385,16,8,128]{3,2,0,1:T(8,128)(2,1)} %bitcast.99), kind=kOutput, calls=%fused_computation.3 | convolution fusion | flops 1620082688 | bytes 25199360 | tf_op jit(solution)/shard_map/fiw,fjw->ijf/dot_general | solution.py:99
  226.7 9.7 %copy.59 = bf16[128,64,384]{2,1,0:T(8,128)(2,1)} copy(bf16[128,64,384]{0,1,2:T(8,128)(2,1)} %fusion) | data formatting | bytes 12582912
  (18 shorter events, 0.2 us)
Async XLA Ops:
  33.7 7.4 %copy-start.1 = (s32[8,64]{1,0:T(8,128)S(1)}, s32[8,64]{1,0:T(8,128)}, u32[]{:S(2)}) copy-start(s32[8,64]{1,0:T(8,128)} %param.9) | copy-start | bytes 6148
  33.7 52.0 %all-to-all-start = ((bf16[16,136,768]{2,1,0:T(8,128)(2,1)}), bf16[16,136,768]{2,1,0:T(8,128)(2,1)S(1)}, u32[]{:S(2)}, u32[]{:S(2)}) async-start(bf16[16,136,768]{2,1,0:T(8,128)(2,1)} %fusion.15), calls=%async_computation | async-start | bytes 6684672 | tf_op jit(solution)/shard_map/all_to_all | solution.py:65
  41.0 146.6 %all-gather.2.cloned.1.call-start = ((), (), s32[]{:S(2)}) async-start(), calls=%async_computation.2 | async-start | bytes 13404160 | tf_op jit(solution)/shard_map/all_gather | solution.py:77
  87.9 3.9 %copy-start = (bf16[1,8,128]{0,2,1:T(8,128)(2,1)S(1)}, bf16[1,8,128]{0,2,1:T(8,128)(2,1)}, u32[]{:S(2)}) copy-start(bf16[1,8,128]{0,2,1:T(8,128)(2,1)} %copy.53) | copy-start | bytes 6148
  98.0 77.7 %all-to-all-start.1 = ((bf16[8,385,8,128]{3,2,1,0:T(8,128)(2,1)}), bf16[8,385,8,128]{3,2,1,0:T(8,128)(2,1)}, u32[]{:S(2)}, u32[]{:S(2)}) async-start(bf16[8,385,8,128]{3,2,1,0:T(8,128)(2,1)} %broadcast_in_dim.130), calls=%async_computation.1 | async-start | bytes 12615680 | tf_op jit(solution)/shard_map/all_to_all | solution.py:83
Sparse Core Ops, SparseCore 0:
  93.5 93.9 all-gather.1

commit v8 on v7

--- a/solution.py
+++ b/solution.py
@@ -34,8 +34,8 @@
     imag = spectrum[:, F:]
     power = (real * real + imag * imag).reshape(count * W, F // BAND, BAND)
     factor = lax.rsqrt(jnp.mean(power, axis=2) + 1e-05)
-    factor = jnp.repeat(factor, BAND, axis=1)
-    white = jnp.concatenate([real * factor, imag * factor], axis=1)
+    factor = jnp.tile(jnp.repeat(factor, BAND, axis=1), (1, 2))
+    white = spectrum * factor
     return white.astype(jnp.bfloat16).reshape(count, W, 2 * F)
 
 
@@ -64,10 +64,12 @@
     payload = jnp.concatenate([payload, label_rows], axis=1)
     arrived = lax.all_to_all(payload, "col", split_axis=0, concat_axis=0, tiled=True)
     tags = arrived[:, CAP * W, :CAP].reshape(outgoing).astype(jnp.int32)
-    flat = arrived[:, : CAP * W, :].reshape(outgoing, W, 2 * F)
     match = tags[None, :] == jnp.arange(owned, dtype=jnp.int32)[:, None]
     pick = jnp.sum(jnp.where(match, jnp.arange(outgoing, dtype=jnp.int32)[None, :], 0), axis=1)
-    spectra = jnp.take(flat, pick, axis=0)
+    block_rows = arrived.shape[1]
+    first_row = pick // CAP * block_rows + pick % CAP * W
+    row_index = first_row[:, None] + jnp.arange(W, dtype=jnp.int32)[None, :]
+    spectra = jnp.take(arrived.reshape(columns * block_rows, 2 * F), row_index, axis=0)
     mask_float = window_mask.astype(jnp.bfloat16)
     spectra = spectra * mask_float[:, :, None]
     stacked = spectra.reshape(owned, W, 2, F).transpose(3, 0, 2, 1).reshape(F, owned, 2 * W)

time: 245 us -> 244 us (level)
    another operation x2 -> x0, local copies, waits for them, and re-layouts: 2.97 us -> none
    unnamed x6 -> x4, local copies, waits for them, and re-layouts: 19.4 us -> 19.4 us
where the time goes in v8:
time: 244 us; the launch traced here: 242 us
  waiting for transfers between devices  121 us (50%)
  local copies, waits for them, and re-layouts  42.9 us (18%)
  matrix products  36.7 us (15%)
  between operations  14.9 us (6%)
  other arithmetic  14.4 us (6%)
  starting transfers between devices  12.6 us (5%)
    all_to_all x1, waiting for transfers between devices, per_device(): got = lax.all_to_all(copies, 'row', split_axis=0, concat_axis=0, tiled=True)  72.4 us
    all_to_all x1, waiting for transfers between devices, per_device(): lax.all_to_all(payload, 'col', split_axis=0, concat_axis=0, tiled=True)  43.7 us
    unnamed x4, local copies, waits for them, and re-layouts  19.4 us
    dot_general x1, matrix products, per_device(): jnp.einsum('fiw,fjw->ijf', left, right, preferred_element_type=jnp.float32)  14.4 us
    dot_general x1, matrix products, per_device(): jnp.einsum('fiw,fjw->ijf', left, turned, preferred_element_type=jnp.float32)  14.1 us
    all_to_all x1, starting transfers between devices, per_device(): lax.all_to_all(payload, 'col', split_axis=0, concat_axis=0, tiled=True)  7.3 us
    dot_general x1, matrix products, whiten(): jnp.dot(segments.reshape(count * W, L), table, preferred_element_type=jnp...  7.29 us
    all_to_all x1, local copies, waits for them, and re-layouts, per_device(): got = lax.all_to_all(copies, 'row', split_axis=0, concat_axis=0, tiled=True)  7.2 us
  transfers between devices with their start and end apart: 3, of which 3 were waited for; matrix products, arithmetic and copies ran while one was open for 5% of the time, Pallas kernels for 0%

profile of v8, /device:TPU:0, one launch (start us, length us, event | category | flops | bytes accessed | tf_op | source)
XLA Modules:
  0.0 242.4 jit_solution(3896039724972708232)
XLA Ops:
  7.8 0.7 fusion.57
  8.5 0.1 fusion.53
  8.6 0.2 select_reduce_fusion.2
  8.8 0.1 select_reduce_fusion.1
  8.9 0.1 reduce_sum.51
  9.0 0.1 broadcast_in_dim.121
  9.1 0.1 broadcast_in_dim.122
  9.2 0.1 convert_element_type.84
  9.3 0.4 fusion.34
  9.7 0.4 fusion.41
  10.1 2.0 subtract_convert_fusion
  12.1 7.3 %fusion.23 = f32[1024,768]{0,1:T(8,128)S(1)} fusion(bf16[1024,3072]{1,0:T(8,128)(2,1)} %bitcast.95, bf16[3072,384]{1,0:T(8,128)(2,1)S(1)} %bitcast.91, bf16[3072,384]{1,0:T(8,128)(2,1)S(1)} %bitcast.90), kind=kOutput, calls=%fused_computation.29 | convolution fusion | flops 4841275392 | bytes 14155776 | tf_op jit(solution)/shard_map/dot_general | solution.py:32
  19.4 1.5 fusion.26
  20.9 1.6 reduce_sum.52
  22.5 0.2 broadcast_in_dim.124
  22.6 1.7 fusion.16
  24.4 1.7 copy.46
  26.1 2.4 gather_fusion
  28.5 2.1 bitcast_select_fusion
  30.6 2.0 fusion.15
  32.6 0.0 copy-start
  32.6 7.3 %all-to-all-start = ((bf16[16,136,768]{2,1,0:T(8,128)(2,1)}), bf16[16,136,768]{2,1,0:T(8,128)(2,1)S(1)}, u32[]{:S(2)}, u32[]{:S(2)}) async-start(bf16[16,136,768]{2,1,0:T(8,128)(2,1)} %fusion.15), calls=%async_computation | async-start | bytes 6684672 | tf_op jit(solution)/shard_map/all_to_all | solution.py:65
  39.9 0.0 all-gather.2.cloned.1.call-start
  40.0 0.0 copy-done
  40.0 0.9 copy.49
  40.9 43.7 %all-to-all-done = bf16[16,136,768]{2,1,0:T(8,128)(2,1)S(1)} async-done(((bf16[16,136,768]{2,1,0:T(8,128)(2,1)}), bf16[16,136,768]{2,1,0:T(8,128)(2,1)S(1)}, u32[]{:S(2)}, u32[]{:S(2)}) %all-to-all-start) | async-done | bytes 3342368 | tf_op jit(solution)/shard_map/all_to_all | solution.py:65
  84.6 0.1 reshape.392
  84.7 0.1 select_reduce_fusion.3
  84.9 0.1 fusion.56
  84.9 0.1 compare_select_fusion.1
  85.0 0.1 reshape.403
  85.1 2.7 %gather_fusion.1 = bf16[512,768]{1,0:T(8,128)(2,1)} fusion(bf16[2176,768]{1,0:T(8,128)(2,1)S(1)} %bitcast.80, s32[1024]{0:T(1024)S(1)} %pad_clamp_fusion), kind=kCustom, calls=%fused_computation.1 | custom fusion | bytes 1574912 | tf_op jit(solution)/shard_map/jit(_take)/gather | solution.py:72
  87.8 2.1 gather.15
  89.9 0.3 fusion.28
  90.1 1.1 pad_maximum_fusion
  91.2 1.4 copy.50
  92.6 0.0 all-gather.2.cloned.1.call-update
  92.6 4.5 %broadcast_in_dim.132 = bf16[8,385,8,128]{3,2,1,0:T(8,128)(2,1)} broadcast(bf16[385,8,128]{2,1,0:T(8,128)(2,1)} %copy.50), dimensions={1,2,3} | broadcast | bytes 7096320 | tf_op jit(solution)/shard_map/broadcast_in_dim | solution.py:84
  97.2 5.3 %all-to-all-start.1 = ((bf16[8,385,8,128]{3,2,1,0:T(8,128)(2,1)}), bf16[8,385,8,128]{3,2,1,0:T(8,128)(2,1)}, u32[]{:S(2)}, u32[]{:S(2)}) async-start(bf16[8,385,8,128]{3,2,1,0:T(8,128)(2,1)} %broadcast_in_dim.132), calls=%async_computation.1 | async-start | bytes 12615680 | tf_op jit(solution)/shard_map/all_to_all | solution.py:85
  102.5 72.4 %all-to-all-done.1 = bf16[8,385,8,128]{3,2,1,0:T(8,128)(2,1)} async-done(((bf16[8,385,8,128]{3,2,1,0:T(8,128)(2,1)}), bf16[8,385,8,128]{3,2,1,0:T(8,128)(2,1)}, u32[]{:S(2)}, u32[]{:S(2)}) %all-to-all-start.1) | async-done | bytes 6307872 | tf_op jit(solution)/shard_map/all_to_all | solution.py:85
  174.9 7.2 %copy.73 = bf16[8,385,8,128]{3,2,0,1:T(8,128)(2,1)} copy(bf16[8,385,8,128]{3,2,1,0:T(8,128)(2,1)} %all-to-all-done.1) | data formatting | bytes 12615680 | tf_op jit(solution)/shard_map/all_to_all | solution.py:85
  182.1 4.7 %all-gather.2.cloned.1.call-done = bf16[49280,128]{1,0:T(8,128)(2,1)} async-done(((bf16[3080,128]{1,0:T(8,128)(2,1)}), bf16[49280,128]{1,0:T(8,128)(2,1)}) %all-gather.2.cloned.1.call-update) | async-done | bytes 12615696 | tf_op jit(solution)/shard_map/all_gather | solution.py:79
  186.8 0.9 fusion.27
  187.7 14.4 %fusion.1 = bf16[128,64,384]{0,1,2:T(8,128)(2,1)} fusion(f32[128,64]{0,1:T(8,128)S(1)} %fusion.27, bf16[385,8,8,128]{3,2,1,0:T(8,128)(2,1)} %bitcast.85, bf16[385,16,8,128]{3,2,0,1:T(8,128)(2,1)} %bitcast.93), kind=kOutput, calls=%fused_computation.5 | convolution fusion | flops 811597824 | bytes 25198592 | tf_op jit(solution)/shard_map/fiw,fjw->ijf/dot_general | solution.py:100
  202.1 9.7 %copy.54 = bf16[128,64,384]{2,1,0:T(8,128)(2,1)} copy(bf16[128,64,384]{0,1,2:T(8,128)(2,1)} %fusion.1) | data formatting | bytes 12582912
  211.8 14.1 %fusion = bf16[128,64,384]{0,1,2:T(8,128)(2,1)} fusion(f32[128,64]{0,1:T(8,128)S(1)} %fusion.27, bf16[385,8,8,128]{3,2,1,0:T(8,128)(2,1)} %bitcast.86, bf16[128]{0:T(256)(128)(2,1)S(1)} %compare_select_fusion.8, s32[128]{0:T(128)S(1)} %and_select_fusion, bf16[385,16,8,128]{3,2,0,1:T(8,128)(2,1)} %bitcast.94), kind=kOutput, calls=%fused_computation.3 | convolution fusion | flops 1620082688 | bytes 25199360 | tf_op jit(solution)/shard_map/fiw,fjw->ijf/dot_general | solution.py:101
  225.9 9.7 %copy.55 = bf16[128,64,384]{2,1,0:T(8,128)(2,1)} copy(bf16[128,64,384]{0,1,2:T(8,128)(2,1)} %fusion) | data formatting | bytes 12582912
  (16 shorter events, 0.2 us)
Async XLA Ops:
  32.6 7.4 %copy-start = (s32[8,64]{1,0:T(8,128)S(1)}, s32[8,64]{1,0:T(8,128)}, u32[]{:S(2)}) copy-start(s32[8,64]{1,0:T(8,128)} %param.9) | copy-start | bytes 6148
  32.6 52.0 %all-to-all-start = ((bf16[16,136,768]{2,1,0:T(8,128)(2,1)}), bf16[16,136,768]{2,1,0:T(8,128)(2,1)S(1)}, u32[]{:S(2)}, u32[]{:S(2)}) async-start(bf16[16,136,768]{2,1,0:T(8,128)(2,1)} %fusion.15), calls=%async_computation | async-start | bytes 6684672 | tf_op jit(solution)/shard_map/all_to_all | solution.py:65
  39.9 146.9 %all-gather.2.cloned.1.call-start = ((), (), s32[]{:S(2)}) async-start(), calls=%async_computation.2 | async-start | bytes 13404160 | tf_op jit(solution)/shard_map/all_gather | solution.py:79
  97.2 77.7 %all-to-all-start.1 = ((bf16[8,385,8,128]{3,2,1,0:T(8,128)(2,1)}), bf16[8,385,8,128]{3,2,1,0:T(8,128)(2,1)}, u32[]{:S(2)}, u32[]{:S(2)}) async-start(bf16[8,385,8,128]{3,2,1,0:T(8,128)(2,1)} %broadcast_in_dim.132), calls=%async_computation.1 | async-start | bytes 12615680 | tf_op jit(solution)/shard_map/all_to_all | solution.py:85
Sparse Core Ops, SparseCore 0:
  92.8 93.9 all-gather.1

commit v9 on v7

--- a/solution.py
+++ b/solution.py
@@ -95,6 +95,7 @@
     turned = jnp.einsum("fjw,wv->fjv", right, swap, preferred_element_type=jnp.float32).astype(
         jnp.bfloat16
     )
+    turned = lax.optimization_barrier(turned)
     real = jnp.einsum("fiw,fjw->ijf", left, right, preferred_element_type=jnp.float32)
     imag = jnp.einsum("fiw,fjw->ijf", left, turned, preferred_element_type=jnp.float32)
     real_part = (real * inverse[:, :, None]).astype(jnp.bfloat16)

time: 245 us -> 245 us (level)
  waiting for transfers between devices: 121 us -> 117 us
  matrix products: 36.7 us -> 40.6 us
    all_gather x1, waiting for transfers between devices: 4.7 us -> 1.04 us  [per_device(): pieces = lax.all_gather(share, 'col', axis=0, tiled=True)]
    dot_general x0 -> x1, matrix products: none -> 3.66 us  [per_device(): jnp.einsum('fjw,wv->fjv', right, swap, preferred_element_type=jnp.float32)]
    all_to_all x1, local copies, waits for them, and re-layouts: 7.2 us -> 4.6 us  [per_device(): got = lax.all_to_all(copies, 'row', split_axis=0, concat_axis=0, tiled=True)]
    unnamed x6 -> x8, local copies, waits for them, and re-layouts: 19.4 us -> 22 us
  transfers between devices with their start and end apart: 3 -> 3, of which waited for: 3 -> 3; matrix products, arithmetic and copies ran while one was open for 5% -> 6% of each run, Pallas kernels for 0% -> 0%
where the time goes in v9:
time: 245 us; the launch traced here: 243 us
  waiting for transfers between devices  117 us (48%)
  local copies, waits for them, and re-layouts  44 us (18%)
  matrix products  40.6 us (17%)
  between operations  14.9 us (6%)
  other arithmetic  14.1 us (6%)
  starting transfers between devices  12.6 us (5%)
    all_to_all x1, waiting for transfers between devices, per_device(): got = lax.all_to_all(copies, 'row', split_axis=0, concat_axis=0, tiled=True)  72.4 us
    all_to_all x1, waiting for transfers between devices, per_device(): lax.all_to_all(payload, 'col', split_axis=0, concat_axis=0, tiled=True)  43.7 us
    unnamed x8, local copies, waits for them, and re-layouts  22 us
    dot_general x1, matrix products, per_device(): jnp.einsum('fiw,fjw->ijf', left, right, preferred_element_type=jnp.float32)  14.4 us
    dot_general x1, matrix products, per_device(): jnp.einsum('fiw,fjw->ijf', left, turned, preferred_element_type=jnp.float32)  14.3 us
    all_to_all x1, starting transfers between devices, per_device(): lax.all_to_all(payload, 'col', split_axis=0, concat_axis=0, tiled=True)  7.3 us
    dot_general x1, matrix products, whiten(): jnp.dot(segments.reshape(count * W, L), table, preferred_element_type=jnp...  7.29 us
    all_to_all x1, starting transfers between devices, per_device(): got = lax.all_to_all(copies, 'row', split_axis=0, concat_axis=0, tiled=True)  5.31 us
  transfers between devices with their start and end apart: 3, of which 3 were waited for; matrix products, arithmetic and copies ran while one was open for 6% of the time, Pallas kernels for 0%

profile of v9, /device:TPU:0, one launch (start us, length us, event | category | flops | bytes accessed | tf_op | source)
XLA Modules:
  0.0 243.4 jit_solution(16661914793292180697)
XLA Ops:
  7.8 0.7 fusion.47
  8.5 0.1 fusion.46
  8.6 0.2 select_reduce_fusion.2
  8.8 0.1 select_reduce_fusion.1
  8.9 0.1 reduce_sum.53
  9.0 0.1 broadcast_in_dim.119
  9.1 0.1 broadcast_in_dim.120
  9.2 0.1 convert_element_type.82
  9.3 0.4 fusion.31
  9.7 0.4 fusion.38
  10.1 2.0 subtract_convert_fusion
  12.1 7.3 %fusion.20 = f32[1024,768]{0,1:T(8,128)S(1)} fusion(bf16[1024,3072]{1,0:T(8,128)(2,1)} %bitcast.96, bf16[3072,384]{1,0:T(8,128)(2,1)S(1)} %bitcast.92, bf16[3072,384]{1,0:T(8,128)(2,1)S(1)} %bitcast.91), kind=kOutput, calls=%fused_computation.29 | convolution fusion | flops 4841275392 | bytes 14155776 | tf_op jit(solution)/shard_map/dot_general | solution.py:32
  19.4 1.5 multiply_add_fusion
  20.9 1.6 reduce_sum.54
  22.5 1.6 fusion.23
  24.0 1.5 copy.49
  25.5 1.5 copy.50
  27.0 0.2 pad_maximum_fusion
  27.2 2.4 gather_fusion
  29.6 2.1 bitcast_select_fusion
  31.7 2.0 fusion.17
  33.7 7.3 %all-to-all-start = ((bf16[16,136,768]{2,1,0:T(8,128)(2,1)}), bf16[16,136,768]{2,1,0:T(8,128)(2,1)S(1)}, u32[]{:S(2)}, u32[]{:S(2)}) async-start(bf16[16,136,768]{2,1,0:T(8,128)(2,1)} %fusion.17), calls=%async_computation | async-start | bytes 6684672 | tf_op jit(solution)/shard_map/all_to_all | solution.py:65
  41.0 0.0 all-gather.2.cloned.1.call-start
  41.0 0.0 copy-done.2
  41.1 0.9 copy.53
  42.0 43.7 %all-to-all-done = bf16[16,136,768]{2,1,0:T(8,128)(2,1)S(1)} async-done(((bf16[16,136,768]{2,1,0:T(8,128)(2,1)}), bf16[16,136,768]{2,1,0:T(8,128)(2,1)S(1)}, u32[]{:S(2)}, u32[]{:S(2)}) %all-to-all-start) | async-done | bytes 3342368 | tf_op jit(solution)/shard_map/all_to_all | solution.py:65
  85.7 0.1 reshape.323
  85.8 0.1 select_reduce_fusion.3
  86.0 2.0 slice.70
  87.9 2.5 %gather_fusion.1 = bf16[8,64,768]{2,1,0:T(8,128)(2,1)S(1)} fusion(bf16[32,64,768]{2,1,0:T(8,128)(2,1)} %bitcast.87, s32[1024]{0:T(1024)S(1)} %pad_clamp_fusion), kind=kCustom, calls=%fused_computation.1 | custom fusion | bytes 1572896 | tf_op jit(solution)/shard_map/jit(_take)/gather | solution.py:70
  90.5 0.2 gather.15
  90.7 1.0 multiply_bitcast_fusion
  91.7 0.1 copy.52
  91.9 0.1 pad_maximum_fusion.1
  92.0 1.4 copy.54
  93.4 0.0 all-gather.2.cloned.1.call-update
  93.4 4.5 %broadcast_in_dim.130 = bf16[8,385,8,128]{3,2,1,0:T(8,128)(2,1)} broadcast(bf16[385,8,128]{2,1,0:T(8,128)(2,1)} %copy.54), dimensions={1,2,3} | broadcast | bytes 7096320 | tf_op jit(solution)/shard_map/broadcast_in_dim | solution.py:82
  98.0 5.3 %all-to-all-start.1 = ((bf16[8,385,8,128]{3,2,1,0:T(8,128)(2,1)}), bf16[8,385,8,128]{3,2,1,0:T(8,128)(2,1)}, u32[]{:S(2)}, u32[]{:S(2)}) async-start(bf16[8,385,8,128]{3,2,1,0:T(8,128)(2,1)} %broadcast_in_dim.130), calls=%async_computation.1 | async-start | bytes 12615680 | tf_op jit(solution)/shard_map/all_to_all | solution.py:83
  103.3 72.4 %all-to-all-done.1 = bf16[8,385,8,128]{3,2,1,0:T(8,128)(2,1)} async-done(((bf16[8,385,8,128]{3,2,1,0:T(8,128)(2,1)}), bf16[8,385,8,128]{3,2,1,0:T(8,128)(2,1)}, u32[]{:S(2)}, u32[]{:S(2)}) %all-to-all-start.1) | async-done | bytes 6307872 | tf_op jit(solution)/shard_map/all_to_all | solution.py:83
  175.7 4.6 %copy.74 = bf16[8,385,8,128]{3,2,0,1:T(8,128)(2,1)S(1)} copy(bf16[8,385,8,128]{3,2,1,0:T(8,128)(2,1)} %all-to-all-done.1) | data formatting | bytes 12615680 | tf_op jit(solution)/shard_map/all_to_all | solution.py:83
  180.3 2.6 %copy-done = bf16[8,385,8,128]{3,2,0,1:T(8,128)(2,1)} copy-done((bf16[8,385,8,128]{3,2,0,1:T(8,128)(2,1)}, bf16[8,385,8,128]{3,2,0,1:T(8,128)(2,1)S(1)}, u32[]{:S(2)}) %copy-start) | copy-done | bytes 6307864
  182.9 3.7 %fusion.16 = bf16[384,64,128]{2,1,0:T(8,128)(2,1)} fusion(bf16[385,8,8,128]{3,2,1,0:T(8,128)(2,1)S(1)} %bitcast.81, bf16[128]{0:T(256)(128)(2,1)S(1)} %compare_select_fusion.8, s32[128]{0:T(128)S(1)} %and_select_fusion), kind=kOutput, calls=%fused_computation.24 | convolution fusion | flops 808484864 | bytes 12583936 | tf_op jit(solution)/shard_map/fjw,wv->fjv/dot_general | solution.py:95
  186.5 1.0 all-gather.2.cloned.1.call-done
  187.6 0.9 fusion.25
  188.5 14.4 %fusion.1 = bf16[128,64,384]{0,1,2:T(8,128)(2,1)} fusion(f32[128,64]{0,1:T(8,128)S(1)} %fusion.25, bf16[385,8,8,128]{3,2,1,0:T(8,128)(2,1)} %bitcast.83, bf16[385,16,8,128]{3,2,0,1:T(8,128)(2,1)} %bitcast.94), kind=kOutput, calls=%fused_computation.5 | convolution fusion | flops 811597824 | bytes 25198592 | tf_op jit(solution)/shard_map/fiw,fjw->ijf/dot_general | solution.py:99
  202.8 9.7 %copy.58 = bf16[128,64,384]{2,1,0:T(8,128)(2,1)} copy(bf16[128,64,384]{0,1,2:T(8,128)(2,1)} %fusion.1) | data formatting | bytes 12582912
  212.5 14.3 %fusion = bf16[128,64,384]{0,1,2:T(8,128)(2,1)} fusion(f32[128,64]{0,1:T(8,128)S(1)} %fusion.25, bf16[384,64,128]{2,1,0:T(8,128)(2,1)} %fusion.16, bf16[385,16,8,128]{3,2,0,1:T(8,128)(2,1)} %bitcast.95), kind=kOutput, calls=%fused_computation.3 | convolution fusion | flops 811597824 | bytes 25198592 | tf_op jit(solution)/shard_map/fiw,fjw->ijf/dot_general | solution.py:100
  226.9 9.7 %copy.59 = bf16[128,64,384]{2,1,0:T(8,128)(2,1)} copy(bf16[128,64,384]{0,1,2:T(8,128)(2,1)} %fusion) | data formatting | bytes 12582912
  (21 shorter events, 0.2 us)
Async XLA Ops:
  33.7 7.4 %copy-start.2 = (s32[8,64]{1,0:T(8,128)S(1)}, s32[8,64]{1,0:T(8,128)}, u32[]{:S(2)}) copy-start(s32[8,64]{1,0:T(8,128)} %param.9) | copy-start | bytes 6148
  33.7 52.0 %all-to-all-start = ((bf16[16,136,768]{2,1,0:T(8,128)(2,1)}), bf16[16,136,768]{2,1,0:T(8,128)(2,1)S(1)}, u32[]{:S(2)}, u32[]{:S(2)}) async-start(bf16[16,136,768]{2,1,0:T(8,128)(2,1)} %fusion.17), calls=%async_computation | async-start | bytes 6684672 | tf_op jit(solution)/shard_map/all_to_all | solution.py:65
  41.0 146.6 %all-gather.2.cloned.1.call-start = ((), (), s32[]{:S(2)}) async-start(), calls=%async_computation.2 | async-start | bytes 13404160 | tf_op jit(solution)/shard_map/all_gather | solution.py:77
  87.9 3.9 %copy-start.1 = (bf16[1,8,128]{0,2,1:T(8,128)(2,1)S(1)}, bf16[1,8,128]{0,2,1:T(8,128)(2,1)}, u32[]{:S(2)}) copy-start(bf16[1,8,128]{0,2,1:T(8,128)(2,1)} %copy.53) | copy-start | bytes 6148
  98.0 77.7 %all-to-all-start.1 = ((bf16[8,385,8,128]{3,2,1,0:T(8,128)(2,1)}), bf16[8,385,8,128]{3,2,1,0:T(8,128)(2,1)}, u32[]{:S(2)}, u32[]{:S(2)}) async-start(bf16[8,385,8,128]{3,2,1,0:T(8,128)(2,1)} %broadcast_in_dim.130), calls=%async_computation.1 | async-start | bytes 12615680 | tf_op jit(solution)/shard_map/all_to_all | solution.py:83
  180.3 2.6 %copy-start = (bf16[8,385,8,128]{3,2,0,1:T(8,128)(2,1)}, bf16[8,385,8,128]{3,2,0,1:T(8,128)(2,1)S(1)}, u32[]{:S(2)}) copy-start(bf16[8,385,8,128]{3,2,0,1:T(8,128)(2,1)S(1)} %copy.74) | copy-start | bytes 18923524
Sparse Core Ops, SparseCore 0:
  93.5 93.9 all-gather.1

commit v10 on v7

--- a/solution.py
+++ b/solution.py
@@ -3,6 +3,7 @@
 import jax
 import jax.numpy as jnp
 from jax import lax
+from jax.experimental.layout import Layout, with_layout_constraint
 from jax.sharding import PartitionSpec as P
 
 F = 384
@@ -95,11 +96,13 @@
     turned = jnp.einsum("fjw,wv->fjv", right, swap, preferred_element_type=jnp.float32).astype(
         jnp.bfloat16
     )
-    real = jnp.einsum("fiw,fjw->ijf", left, right, preferred_element_type=jnp.float32)
-    imag = jnp.einsum("fiw,fjw->ijf", left, turned, preferred_element_type=jnp.float32)
-    real_part = (real * inverse[:, :, None]).astype(jnp.bfloat16)
-    imag_part = (imag * inverse[:, :, None]).astype(jnp.bfloat16)
-    return (real_part, imag_part)
+    across = right.shape[1]
+    both = jnp.concatenate([right, turned], axis=1)
+    product = jnp.einsum("fiw,fjw->fij", left, both, preferred_element_type=jnp.float32)
+    scale = jnp.concatenate([inverse, inverse], axis=1)
+    product = (product * scale[None]).astype(jnp.bfloat16)
+    product = with_layout_constraint(product, Layout((0, 1, 2)))
+    return (product[:, :, :across].transpose(1, 2, 0), product[:, :, across:].transpose(1, 2, 0))
 
 
 def solution(mesh):

time: 245 us -> 271 us (1.11)
  local copies, waits for them, and re-layouts: 44 us -> 80 us
  matrix products: 36.7 us -> 29.9 us
  waiting for transfers between devices: 121 us -> 116 us
    transpose x0 -> x1, local copies, waits for them, and re-layouts: none -> 20 us  [per_device(): product[:, :, across:].transpose(1, 2, 0)]
    unnamed x6 -> x8, local copies, waits for them, and re-layouts: 19.4 us -> 33.1 us
    dot_general x2, matrix products: 28.5 us -> 21.7 us  [the longest x1 18 us: per_device(): jnp.einsum('fiw,fjw->fij', left, both, preferred_element_type=jnp.float32)]
    slice x0 -> x1, local copies, waits for them, and re-layouts: none -> 4.77 us  [per_device(): right, right_mask = (right_all[:F], right_all[F, :, :W])]
    all_gather x1, waiting for transfers between devices: 4.7 us -> 0.01 us  [per_device(): pieces = lax.all_gather(share, 'col', axis=0, tiled=True)]
  transfers between devices with their start and end apart: 3 -> 3, of which waited for: 3 -> 2; matrix products, arithmetic and copies ran while one was open for 5% -> 7% of each run, Pallas kernels for 0% -> 0%
where the time goes in v10:
time: 271 us; the launch traced here: 268 us
  waiting for transfers between devices  116 us (43%)
  local copies, waits for them, and re-layouts  80 us (30%)
  matrix products  29.9 us (11%)
  between operations  14.9 us (5%)
  other arithmetic  14.1 us (5%)
  starting transfers between devices  12.6 us (5%)
    all_to_all x1, waiting for transfers between devices, per_device(): got = lax.all_to_all(copies, 'row', split_axis=0, concat_axis=0, tiled=True)  72.4 us
    all_to_all x1, waiting for transfers between devices, per_device(): lax.all_to_all(payload, 'col', split_axis=0, concat_axis=0, tiled=True)  43.7 us
    unnamed x8, local copies, waits for them, and re-layouts  33.1 us
    transpose x1, local copies, waits for them, and re-layouts, per_device(): product[:, :, across:].transpose(1, 2, 0)  20 us
    dot_general x1, matrix products, per_device(): jnp.einsum('fiw,fjw->fij', left, both, preferred_element_type=jnp.float32)  18 us
    all_to_all x1, starting transfers between devices, per_device(): lax.all_to_all(payload, 'col', split_axis=0, concat_axis=0, tiled=True)  7.3 us
    dot_general x1, matrix products, whiten(): jnp.dot(segments.reshape(count * W, L), table, preferred_element_type=jnp...  7.29 us
  transfers between devices with their start and end apart: 3, of which 2 were waited for; matrix products, arithmetic and copies ran while one was open for 7% of the time, Pallas kernels for 0%

profile of v10, /device:TPU:0, one launch (start us, length us, event | category | flops | bytes accessed | tf_op | source)
XLA Modules:
  0.0 267.7 jit_solution(2538753694187425532)
XLA Ops:
  7.8 0.7 fusion.43
  8.5 0.1 fusion.42
  8.6 0.2 select_reduce_fusion.2
  8.8 0.1 select_reduce_fusion.1
  8.9 0.1 reduce_sum.53
  9.0 0.1 broadcast_in_dim.118
  9.1 0.1 broadcast_in_dim.119
  9.2 0.1 convert_element_type.78
  9.3 0.4 fusion.27
  9.7 0.4 fusion.34
  10.1 2.0 subtract_convert_fusion
  12.1 7.3 %fusion.16 = f32[1024,768]{0,1:T(8,128)S(1)} fusion(bf16[1024,3072]{1,0:T(8,128)(2,1)} %bitcast.81, bf16[3072,384]{1,0:T(8,128)(2,1)S(1)} %bitcast.78, bf16[3072,384]{1,0:T(8,128)(2,1)S(1)} %bitcast.77), kind=kOutput, calls=%fused_computation.27 | convolution fusion | flops 4841275392 | bytes 14155776 | tf_op jit(solution)/shard_map/dot_general | solution.py:33
  19.4 1.5 multiply_add_fusion
  20.9 1.6 reduce_sum.54
  22.5 1.6 fusion.19
  24.0 1.5 copy.54
  25.5 1.5 copy.55
  27.0 0.2 pad_maximum_fusion
  27.2 2.4 gather_fusion
  29.6 2.1 bitcast_select_fusion
  31.7 2.0 fusion.15
  33.7 7.3 %all-to-all-start = ((bf16[16,136,768]{2,1,0:T(8,128)(2,1)}), bf16[16,136,768]{2,1,0:T(8,128)(2,1)S(1)}, u32[]{:S(2)}, u32[]{:S(2)}) async-start(bf16[16,136,768]{2,1,0:T(8,128)(2,1)} %fusion.15), calls=%async_computation | async-start | bytes 6684672 | tf_op jit(solution)/shard_map/all_to_all | solution.py:66
  41.0 0.0 all-gather.2.cloned.1.call-start
  41.0 0.0 copy-done.2
  41.1 0.9 copy.58
  42.0 43.7 %all-to-all-done = bf16[16,136,768]{2,1,0:T(8,128)(2,1)S(1)} async-done(((bf16[16,136,768]{2,1,0:T(8,128)(2,1)}), bf16[16,136,768]{2,1,0:T(8,128)(2,1)S(1)}, u32[]{:S(2)}, u32[]{:S(2)}) %all-to-all-start) | async-done | bytes 3342368 | tf_op jit(solution)/shard_map/all_to_all | solution.py:66
  85.7 0.1 reshape.323
  85.8 0.1 select_reduce_fusion.3
  86.0 2.0 slice.78
  87.9 2.5 gather_fusion.1
  90.5 0.2 gather.15
  90.7 1.0 multiply_bitcast_fusion
  91.7 0.1 copy.57
  91.9 0.1 pad_maximum_fusion.1
  92.0 1.4 copy.59
  93.4 0.0 all-gather.2.cloned.1.call-update
  93.5 4.5 %broadcast_in_dim.129 = bf16[8,385,8,128]{3,2,1,0:T(8,128)(2,1)} broadcast(bf16[385,8,128]{2,1,0:T(8,128)(2,1)} %copy.59), dimensions={1,2,3} | broadcast | bytes 7096320 | tf_op jit(solution)/shard_map/broadcast_in_dim | solution.py:83
  98.0 5.3 %all-to-all-start.1 = ((bf16[8,385,8,128]{3,2,1,0:T(8,128)(2,1)}), bf16[8,385,8,128]{3,2,1,0:T(8,128)(2,1)}, u32[]{:S(2)}, u32[]{:S(2)}) async-start(bf16[8,385,8,128]{3,2,1,0:T(8,128)(2,1)} %broadcast_in_dim.129), calls=%async_computation.1 | async-start | bytes 12615680 | tf_op jit(solution)/shard_map/all_to_all | solution.py:84
  103.3 72.4 %all-to-all-done.1 = bf16[8,385,8,128]{3,2,1,0:T(8,128)(2,1)} async-done(((bf16[8,385,8,128]{3,2,1,0:T(8,128)(2,1)}), bf16[8,385,8,128]{3,2,1,0:T(8,128)(2,1)}, u32[]{:S(2)}, u32[]{:S(2)}) %all-to-all-start.1) | async-done | bytes 6307872 | tf_op jit(solution)/shard_map/all_to_all | solution.py:84
  175.7 4.6 %copy.74 = bf16[8,385,8,128]{3,2,0,1:T(8,128)(2,1)S(1)} copy(bf16[8,385,8,128]{3,2,1,0:T(8,128)(2,1)} %all-to-all-done.1) | data formatting | bytes 12615680 | tf_op jit(solution)/shard_map/all_to_all | solution.py:84
  180.3 4.8 %slice_bitcast_fusion.2 = bf16[384,64,128]{2,1,0:T(8,128)(2,1)} fusion(bf16[385,8,8,128]{3,2,1,0:T(8,128)(2,1)S(1)} %bitcast.67), kind=kLoop, calls=%fused_computation.13 | loop fusion | bytes 12582912 | tf_op jit(solution)/shard_map/slice | solution.py:87
  185.1 3.7 %convolution_convert_fusion = bf16[384,64,128]{2,1,0:T(8,128)(2,1)} fusion(bf16[128]{0:T(256)(128)(2,1)S(1)} %compare_select_fusion.8, s32[128]{0:T(128)S(1)} %and_select_fusion, bf16[385,8,8,128]{3,2,1,0:T(8,128)(2,1)S(1)} %bitcast.68), kind=kOutput, calls=%fused_computation.22 | convolution fusion | flops 808484864 | bytes 12583936 | tf_op jit(solution)/shard_map/fjw,wv->fjv/dot_general | solution.py:96
  188.8 0.9 fusion.21
  189.7 0.1 copy.63
  189.8 18.0 %multiply_convert_fusion = bf16[384,128,128]{2,1,0:T(8,128)(2,1)} fusion(f32[128,128]{1,0:T(8,128)S(1)} %copy.63, bf16[384,64,128]{2,1,0:T(8,128)(2,1)} %convolution_convert_fusion, bf16[384,64,128]{2,1,0:T(8,128)(2,1)} %slice_bitcast_fusion.2, bf16[385,16,8,128]{3,2,0,1:T(8,128)(2,1)} %bitcast.80), kind=kOutput, calls=%fused_computation.2 | convolution fusion | flops 1648361472 | bytes 37814272 | tf_op jit(solution)/shard_map/fiw,fjw->fij/dot_general | solution.py:101
  207.8 20.0 %slice_bitcast_fusion = (bf16[128,64,384]{1,0,2:T(8,128)(2,1)}, bf16[128,64,384]{1,0,2:T(8,128)(2,1)}) fusion(bf16[384,128,128]{2,1,0:T(8,128)(2,1)} %multiply_convert_fusion), kind=kLoop, calls=%fused_computation.3 | loop fusion | bytes 25165824 | tf_op jit(solution)/shard_map/transpose | solution.py:105
  227.7 16.5 %copy.65 = bf16[128,64,384]{2,1,0:T(8,128)(2,1)} copy(bf16[128,64,384]{1,0,2:T(8,128)(2,1)} %get-tuple-element.28) | data formatting | bytes 12582912
  244.3 16.5 %copy.64 = bf16[128,64,384]{2,1,0:T(8,128)(2,1)} copy(bf16[128,64,384]{1,0,2:T(8,128)(2,1)} %get-tuple-element.29) | data formatting | bytes 12582912
  (24 shorter events, 0.2 us)
Async XLA Ops:
  33.7 7.4 %copy-start.2 = (s32[8,64]{1,0:T(8,128)S(1)}, s32[8,64]{1,0:T(8,128)}, u32[]{:S(2)}) copy-start(s32[8,64]{1,0:T(8,128)} %param.9) | copy-start | bytes 6148
  33.7 52.0 %all-to-all-start = ((bf16[16,136,768]{2,1,0:T(8,128)(2,1)}), bf16[16,136,768]{2,1,0:T(8,128)(2,1)S(1)}, u32[]{:S(2)}, u32[]{:S(2)}) async-start(bf16[16,136,768]{2,1,0:T(8,128)(2,1)} %fusion.15), calls=%async_computation | async-start | bytes 6684672 | tf_op jit(solution)/shard_map/all_to_all | solution.py:66
  41.0 147.8 %all-gather.2.cloned.1.call-start = ((), (), s32[]{:S(2)}) async-start(), calls=%async_computation.2 | async-start | bytes 13404160 | tf_op jit(solution)/shard_map/all_gather | solution.py:78
  87.9 3.9 %copy-start.1 = (bf16[1,8,128]{0,2,1:T(8,128)(2,1)S(1)}, bf16[1,8,128]{0,2,1:T(8,128)(2,1)}, u32[]{:S(2)}) copy-start(bf16[1,8,128]{0,2,1:T(8,128)(2,1)} %copy.58) | copy-start | bytes 6148
  98.0 77.7 %all-to-all-start.1 = ((bf16[8,385,8,128]{3,2,1,0:T(8,128)(2,1)}), bf16[8,385,8,128]{3,2,1,0:T(8,128)(2,1)}, u32[]{:S(2)}, u32[]{:S(2)}) async-start(bf16[8,385,8,128]{3,2,1,0:T(8,128)(2,1)} %broadcast_in_dim.129), calls=%async_computation.1 | async-start | bytes 12615680 | tf_op jit(solution)/shard_map/all_to_all | solution.py:84
  180.3 4.8 %copy-start = (bf16[8,385,8,128]{3,2,0,1:T(8,128)(2,1)}, bf16[8,385,8,128]{3,2,0,1:T(8,128)(2,1)S(1)}, u32[]{:S(2)}) copy-start(bf16[8,385,8,128]{3,2,0,1:T(8,128)(2,1)S(1)} %copy.74) | copy-start | bytes 18923524
Sparse Core Ops, SparseCore 0:
  93.6 93.9 all-gather.1

commit v11 on v8

--- a/solution.py
+++ b/solution.py
@@ -97,6 +97,7 @@
     turned = jnp.einsum("fjw,wv->fjv", right, swap, preferred_element_type=jnp.float32).astype(
         jnp.bfloat16
     )
+    turned = lax.optimization_barrier(turned)
     real = jnp.einsum("fiw,fjw->ijf", left, right, preferred_element_type=jnp.float32)
     imag = jnp.einsum("fiw,fjw->ijf", left, turned, preferred_element_type=jnp.float32)
     real_part = (real * inverse[:, :, None]).astype(jnp.bfloat16)

time: 244 us -> 244 us (level)
  waiting for transfers between devices: 121 us -> 117 us
  matrix products: 36.7 us -> 40.6 us
    all_gather x1, waiting for transfers between devices: 4.7 us -> 1.05 us  [per_device(): pieces = lax.all_gather(share, 'col', axis=0, tiled=True)]
    dot_general x0 -> x1, matrix products: none -> 3.65 us  [per_device(): jnp.einsum('fjw,wv->fjv', right, swap, preferred_element_type=jnp.float32)]
    all_to_all x1, local copies, waits for them, and re-layouts: 7.2 us -> 4.6 us  [per_device(): got = lax.all_to_all(copies, 'row', split_axis=0, concat_axis=0, tiled=True)]
    unnamed x4 -> x6, local copies, waits for them, and re-layouts: 19.4 us -> 22 us
  transfers between devices with their start and end apart: 3 -> 3, of which waited for: 3 -> 3; matrix products, arithmetic and copies ran while one was open for 5% -> 6% of each run, Pallas kernels for 0% -> 0%
where the time goes in v11:
time: 244 us; the launch traced here: 243 us
  waiting for transfers between devices  117 us (48%)
  local copies, waits for them, and re-layouts  42.9 us (18%)
  matrix products  40.6 us (17%)
  between operations  14.9 us (6%)
  other arithmetic  14.4 us (6%)
  starting transfers between devices  12.6 us (5%)
    all_to_all x1, waiting for transfers between devices, per_device(): got = lax.all_to_all(copies, 'row', split_axis=0, concat_axis=0, tiled=True)  72.4 us
    all_to_all x1, waiting for transfers between devices, per_device(): lax.all_to_all(payload, 'col', split_axis=0, concat_axis=0, tiled=True)  43.7 us
    unnamed x6, local copies, waits for them, and re-layouts  22 us
    dot_general x1, matrix products, per_device(): jnp.einsum('fiw,fjw->ijf', left, right, preferred_element_type=jnp.float32)  14.4 us
    dot_general x1, matrix products, per_device(): jnp.einsum('fiw,fjw->ijf', left, turned, preferred_element_type=jnp.float32)  14.3 us
    all_to_all x1, starting transfers between devices, per_device(): lax.all_to_all(payload, 'col', split_axis=0, concat_axis=0, tiled=True)  7.3 us
    dot_general x1, matrix products, whiten(): jnp.dot(segments.reshape(count * W, L), table, preferred_element_type=jnp...  7.29 us
    all_to_all x1, starting transfers between devices, per_device(): got = lax.all_to_all(copies, 'row', split_axis=0, concat_axis=0, tiled=True)  5.31 us
  transfers between devices with their start and end apart: 3, of which 3 were waited for; matrix products, arithmetic and copies ran while one was open for 6% of the time, Pallas kernels for 0%

profile of v11, /device:TPU:0, one launch (start us, length us, event | category | flops | bytes accessed | tf_op | source)
XLA Modules:
  0.0 242.6 jit_solution(18211217018925543315)
XLA Ops:
  7.8 0.7 fusion.51
  8.5 0.1 fusion.47
  8.6 0.2 select_reduce_fusion.2
  8.8 0.1 select_reduce_fusion.1
  8.9 0.1 reduce_sum.51
  9.0 0.1 broadcast_in_dim.121
  9.1 0.1 broadcast_in_dim.122
  9.2 0.1 convert_element_type.84
  9.3 0.4 fusion.32
  9.7 0.4 fusion.39
  10.1 2.0 subtract_convert_fusion
  12.1 7.3 %fusion.21 = f32[1024,768]{0,1:T(8,128)S(1)} fusion(bf16[1024,3072]{1,0:T(8,128)(2,1)} %bitcast.91, bf16[3072,384]{1,0:T(8,128)(2,1)S(1)} %bitcast.87, bf16[3072,384]{1,0:T(8,128)(2,1)S(1)} %bitcast.86), kind=kOutput, calls=%fused_computation.29 | convolution fusion | flops 4841275392 | bytes 14155776 | tf_op jit(solution)/shard_map/dot_general | solution.py:32
  19.4 1.5 fusion.24
  20.9 1.6 reduce_sum.52
  22.5 0.2 broadcast_in_dim.124
  22.6 1.7 fusion.18
  24.4 1.7 copy.46
  26.1 2.4 gather_fusion
  28.5 2.1 bitcast_select_fusion
  30.6 2.0 fusion.17
  32.6 7.3 %all-to-all-start = ((bf16[16,136,768]{2,1,0:T(8,128)(2,1)}), bf16[16,136,768]{2,1,0:T(8,128)(2,1)S(1)}, u32[]{:S(2)}, u32[]{:S(2)}) async-start(bf16[16,136,768]{2,1,0:T(8,128)(2,1)} %fusion.17), calls=%async_computation | async-start | bytes 6684672 | tf_op jit(solution)/shard_map/all_to_all | solution.py:65
  39.9 0.0 all-gather.2.cloned.1.call-start
  40.0 0.0 copy-done.1
  40.0 0.9 copy.49
  40.9 43.7 %all-to-all-done = bf16[16,136,768]{2,1,0:T(8,128)(2,1)S(1)} async-done(((bf16[16,136,768]{2,1,0:T(8,128)(2,1)}), bf16[16,136,768]{2,1,0:T(8,128)(2,1)S(1)}, u32[]{:S(2)}, u32[]{:S(2)}) %all-to-all-start) | async-done | bytes 3342368 | tf_op jit(solution)/shard_map/all_to_all | solution.py:65
  84.6 0.1 reshape.392
  84.7 0.1 select_reduce_fusion.3
  84.9 0.1 fusion.50
  84.9 0.1 compare_select_fusion.1
  85.0 0.1 reshape.403
  85.1 2.7 %gather_fusion.1 = bf16[512,768]{1,0:T(8,128)(2,1)} fusion(bf16[2176,768]{1,0:T(8,128)(2,1)S(1)} %bitcast.76, s32[1024]{0:T(1024)S(1)} %pad_clamp_fusion), kind=kCustom, calls=%fused_computation.1 | custom fusion | bytes 1574912 | tf_op jit(solution)/shard_map/jit(_take)/gather | solution.py:72
  87.8 2.1 gather.15
  89.9 0.3 fusion.26
  90.1 1.1 pad_maximum_fusion
  91.2 1.4 copy.50
  92.6 0.0 all-gather.2.cloned.1.call-update
  92.6 4.5 %broadcast_in_dim.132 = bf16[8,385,8,128]{3,2,1,0:T(8,128)(2,1)} broadcast(bf16[385,8,128]{2,1,0:T(8,128)(2,1)} %copy.50), dimensions={1,2,3} | broadcast | bytes 7096320 | tf_op jit(solution)/shard_map/broadcast_in_dim | solution.py:84
  97.2 5.3 %all-to-all-start.1 = ((bf16[8,385,8,128]{3,2,1,0:T(8,128)(2,1)}), bf16[8,385,8,128]{3,2,1,0:T(8,128)(2,1)}, u32[]{:S(2)}, u32[]{:S(2)}) async-start(bf16[8,385,8,128]{3,2,1,0:T(8,128)(2,1)} %broadcast_in_dim.132), calls=%async_computation.1 | async-start | bytes 12615680 | tf_op jit(solution)/shard_map/all_to_all | solution.py:85
  102.5 72.4 %all-to-all-done.1 = bf16[8,385,8,128]{3,2,1,0:T(8,128)(2,1)} async-done(((bf16[8,385,8,128]{3,2,1,0:T(8,128)(2,1)}), bf16[8,385,8,128]{3,2,1,0:T(8,128)(2,1)}, u32[]{:S(2)}, u32[]{:S(2)}) %all-to-all-start.1) | async-done | bytes 6307872 | tf_op jit(solution)/shard_map/all_to_all | solution.py:85
  174.9 4.6 %copy.73 = bf16[8,385,8,128]{3,2,0,1:T(8,128)(2,1)S(1)} copy(bf16[8,385,8,128]{3,2,1,0:T(8,128)(2,1)} %all-to-all-done.1) | data formatting | bytes 12615680 | tf_op jit(solution)/shard_map/all_to_all | solution.py:85
  179.5 2.6 %copy-done = bf16[8,385,8,128]{3,2,0,1:T(8,128)(2,1)} copy-done((bf16[8,385,8,128]{3,2,0,1:T(8,128)(2,1)}, bf16[8,385,8,128]{3,2,0,1:T(8,128)(2,1)S(1)}, u32[]{:S(2)}) %copy-start) | copy-done | bytes 6307864
  182.1 3.6 %fusion.16 = bf16[384,64,128]{2,1,0:T(8,128)(2,1)} fusion(bf16[385,8,8,128]{3,2,1,0:T(8,128)(2,1)S(1)} %bitcast.77, bf16[128]{0:T(256)(128)(2,1)S(1)} %compare_select_fusion.8, s32[128]{0:T(128)S(1)} %and_select_fusion), kind=kOutput, calls=%fused_computation.24 | convolution fusion | flops 808484864 | bytes 12583936 | tf_op jit(solution)/shard_map/fjw,wv->fjv/dot_general | solution.py:97
  185.7 1.0 all-gather.2.cloned.1.call-done
  186.8 0.9 fusion.25
  187.7 14.4 %fusion.1 = bf16[128,64,384]{0,1,2:T(8,128)(2,1)} fusion(f32[128,64]{0,1:T(8,128)S(1)} %fusion.25, bf16[385,8,8,128]{3,2,1,0:T(8,128)(2,1)} %bitcast.79, bf16[385,16,8,128]{3,2,0,1:T(8,128)(2,1)} %bitcast.89), kind=kOutput, calls=%fused_computation.5 | convolution fusion | flops 811597824 | bytes 25198592 | tf_op jit(solution)/shard_map/fiw,fjw->ijf/dot_general | solution.py:101
  202.1 9.7 %copy.54 = bf16[128,64,384]{2,1,0:T(8,128)(2,1)} copy(bf16[128,64,384]{0,1,2:T(8,128)(2,1)} %fusion.1) | data formatting | bytes 12582912
  211.8 14.3 %fusion = bf16[128,64,384]{0,1,2:T(8,128)(2,1)} fusion(f32[128,64]{0,1:T(8,128)S(1)} %fusion.25, bf16[384,64,128]{2,1,0:T(8,128)(2,1)} %fusion.16, bf16[385,16,8,128]{3,2,0,1:T(8,128)(2,1)} %bitcast.90), kind=kOutput, calls=%fused_computation.3 | convolution fusion | flops 811597824 | bytes 25198592 | tf_op jit(solution)/shard_map/fiw,fjw->ijf/dot_general | solution.py:102
  226.1 9.7 %copy.55 = bf16[128,64,384]{2,1,0:T(8,128)(2,1)} copy(bf16[128,64,384]{0,1,2:T(8,128)(2,1)} %fusion) | data formatting | bytes 12582912
  (18 shorter events, 0.2 us)
Async XLA Ops:
  32.6 7.4 %copy-start.1 = (s32[8,64]{1,0:T(8,128)S(1)}, s32[8,64]{1,0:T(8,128)}, u32[]{:S(2)}) copy-start(s32[8,64]{1,0:T(8,128)} %param.9) | copy-start | bytes 6148
  32.6 52.0 %all-to-all-start = ((bf16[16,136,768]{2,1,0:T(8,128)(2,1)}), bf16[16,136,768]{2,1,0:T(8,128)(2,1)S(1)}, u32[]{:S(2)}, u32[]{:S(2)}) async-start(bf16[16,136,768]{2,1,0:T(8,128)(2,1)} %fusion.17), calls=%async_computation | async-start | bytes 6684672 | tf_op jit(solution)/shard_map/all_to_all | solution.py:65
  39.9 146.9 %all-gather.2.cloned.1.call-start = ((), (), s32[]{:S(2)}) async-start(), calls=%async_computation.2 | async-start | bytes 13404160 | tf_op jit(solution)/shard_map/all_gather | solution.py:79
  97.2 77.7 %all-to-all-start.1 = ((bf16[8,385,8,128]{3,2,1,0:T(8,128)(2,1)}), bf16[8,385,8,128]{3,2,1,0:T(8,128)(2,1)}, u32[]{:S(2)}, u32[]{:S(2)}) async-start(bf16[8,385,8,128]{3,2,1,0:T(8,128)(2,1)} %broadcast_in_dim.132), calls=%async_computation.1 | async-start | bytes 12615680 | tf_op jit(solution)/shard_map/all_to_all | solution.py:85
  179.5 2.6 %copy-start = (bf16[8,385,8,128]{3,2,0,1:T(8,128)(2,1)}, bf16[8,385,8,128]{3,2,0,1:T(8,128)(2,1)S(1)}, u32[]{:S(2)}) copy-start(bf16[8,385,8,128]{3,2,0,1:T(8,128)(2,1)S(1)} %copy.73) | copy-start | bytes 18923524
Sparse Core Ops, SparseCore 0:
  92.8 93.9 all-gather.1
